TPU v7x, 512 devices: a whole 4x8x8 slice. The times are simulated.
512 devices in a mesh: ens: 16 (over z, x_hi), tile: 32 (over y, x_lo, core).
Axes of the slice: x: 4 (x_hi: 2, x_lo: 2; x = x_hi * 2 + x_lo), y: 8, z: 8, core: 2. Of those that a mesh axis runs over, the one named last changes fastest.
Arguments:
- conditioning: bfloat16 [12, 256, 128], P(None, 'tile'), may hold values from -6 to 6
- member_noise: float32 [16, 4, 256, 128], P('ens', None, 'tile'), may hold values from -6 to 6
- reg_in: bfloat16 [3, 3, 12, 128], replicated, may hold values from -1 to 1
- reg_down: bfloat16 [3, 3, 128, 128], replicated, may hold values from -0.25 to 0.25
- reg_low: bfloat16 [3, 3, 128, 128], replicated, may hold values from -0.25 to 0.25
- reg_up: bfloat16 [4, 4, 128, 128], replicated, may hold values from -0.375 to 0.375
- reg_fine: bfloat16 [3, 3, 128, 128], replicated, may hold values from -0.25 to 0.25
- reg_out: bfloat16 [3, 3, 4, 128], replicated, may hold values from -0.3125 to 0.3125
- dif_in: bfloat16 [3, 3, 20, 128], replicated, may hold values from -0.75 to 0.75
- dif_down: bfloat16 [3, 3, 128, 128], replicated, may hold values from -0.25 to 0.25
- dif_low: bfloat16 [3, 3, 128, 128], replicated, may hold values from -0.25 to 0.25
- dif_up: bfloat16 [4, 4, 128, 128], replicated, may hold values from -0.375 to 0.375
- dif_fine: bfloat16 [3, 3, 128, 128], replicated, may hold values from -0.25 to 0.25
- dif_out: bfloat16 [3, 3, 4, 128], replicated, may hold values from -0.3125 to 0.3125
Outputs:
- prediction: float32 [16, 4, 256, 128], P('ens', None, 'tile')
All inputs are finite; a program needn't handle non-finite values.
Results may differ from a plain program's by a relative error of at most 0.015.
Values may be sent and summed in bfloat16 or wider, within the bound.
No kernel may reach another device: no remote copies, remote signals or barrier semaphores. Data moves between devices by JAX's collectives and lax.ppermute only.
A program may use at most 64 MiB of HBM per device.

v0:
```python
import jax
import jax.numpy as jnp
from jax import lax
from jax.sharding import PartitionSpec as P

STEPS = 2
sigma_top = 1.0
sigma_ratio = 0.4
sigma_data = 0.5


def with_halo(cells, sides, width):
    for axis, dim in sides:
        count = lax.axis_size(axis)
        ends = count - 1
        head = lax.slice_in_dim(cells, 0, width, axis=dim)
        tail = lax.slice_in_dim(cells, cells.shape[dim] - width, cells.shape[dim], axis=dim)
        cells = jnp.concatenate(
            [
                lax.ppermute(tail, axis, [(i, (i + 1) % count) for i in range(ends)]),
                cells,
                lax.ppermute(head, axis, [((i + 1) % count, i) for i in range(ends)]),
            ],
            axis=dim,
        )
    return cells


def silu_round(values):
    return jax.nn.silu(values).astype(jnp.bfloat16)


def conv_fields(padded, weight):
    height = padded.shape[1] - 2
    across = padded.shape[2] - 2
    running = None
    for tap_y in range(3):
        for tap_x in range(3):
            window = padded[:, tap_y : tap_y + height, tap_x : tap_x + across]
            tap_term = jnp.einsum(
                "crw,co->rwo", window, weight[tap_y, tap_x], preferred_element_type=jnp.float32
            )
            running = tap_term if running is None else running + tap_term
    return running


def conv_feat(padded, weight, stride):
    count_y = (padded.shape[0] - 3) // stride + 1
    count_x = (padded.shape[1] - 3) // stride + 1
    running = None
    for tap_y in range(3):
        for tap_x in range(3):
            window = padded[
                tap_y : tap_y + stride * (count_y - 1) + 1 : stride,
                tap_x : tap_x + stride * (count_x - 1) + 1 : stride,
            ]
            tap_term = jnp.dot(window, weight[tap_y, tap_x], preferred_element_type=jnp.float32)
            running = tap_term if running is None else running + tap_term
    return running


def conv_out(padded, weight):
    height = padded.shape[0] - 2
    across = padded.shape[1] - 2
    running = None
    for tap_y in range(3):
        for tap_x in range(3):
            window = padded[tap_y : tap_y + height, tap_x : tap_x + across]
            tap_term = jnp.einsum(
                "rwc,oc->orw", window, weight[tap_y, tap_x], preferred_element_type=jnp.float32
            )
            running = tap_term if running is None else running + tap_term
    return running


def up_conv(padded, weight):
    count_y = padded.shape[0] - 2
    count_x = padded.shape[1] - 2
    tap_pairs = (((1, 1), (0, 3)), ((2, 0), (1, 2)))

    def parity(side_y, side_x):
        running = None
        for offset_y, kernel_y in tap_pairs[side_y]:
            for offset_x, kernel_x in tap_pairs[side_x]:
                window = padded[offset_y : offset_y + count_y, offset_x : offset_x + count_x]
                tap_term = jnp.dot(
                    window, weight[kernel_y, kernel_x], preferred_element_type=jnp.float32
                )
                running = tap_term if running is None else running + tap_term
        return running

    upper_rows = jnp.stack([parity(0, 0), parity(0, 1)], axis=2)
    lower_rows = jnp.stack([parity(1, 0), parity(1, 1)], axis=2)
    merged = jnp.stack([upper_rows, lower_rows], axis=1)
    return merged.reshape(2 * count_y, 2 * count_x, merged.shape[-1])


def col_pad(values):
    return jnp.pad(values, ((0, 0), (1, 1), (0, 0)))


def feat_pad(values):
    return col_pad(with_halo(values, (("tile", 0),), 1))


def strip_pad(values):
    return with_halo(values, (("ens", 1), ("tile", 0)), 1)


def lower_each(top_level, down_weight, low_weight, up_weight, pad_fn):
    coarse = silu_round(conv_feat(pad_fn(top_level), down_weight, 2))
    middle = silu_round(conv_feat(pad_fn(coarse), low_weight, 1))
    return up_conv(pad_fn(middle), up_weight)


def network_pass(padded_fields, weights, pad_fn, lower_fn):
    in_weight, down_weight, low_weight, up_weight, fine_weight, out_weight = weights
    top_level = silu_round(conv_fields(padded_fields, in_weight))
    upward = lower_fn(top_level, down_weight, low_weight, up_weight, pad_fn)
    summed = (top_level.astype(jnp.float32) + upward).astype(jnp.bfloat16)
    refined = silu_round(conv_feat(pad_fn(summed), fine_weight, 1))
    return conv_out(pad_fn(refined), out_weight)


def shards(
    conditioning,
    member_noise,
    reg_in,
    reg_down,
    reg_low,
    reg_up,
    reg_fine,
    reg_out,
    dif_in,
    dif_down,
    dif_low,
    dif_up,
    dif_fine,
    dif_out,
):
    grid_cols = conditioning.shape[2]
    reg_weights = (reg_in, reg_down, reg_low, reg_up, reg_fine, reg_out)
    dif_weights = (dif_in, dif_down, dif_low, dif_up, dif_fine, dif_out)
    cond_rows = with_halo(conditioning, (("tile", 1),), 1)
    cond_padded = jnp.pad(cond_rows, ((0, 0), (0, 0), (1, 1)))
    strip_width = grid_cols // lax.axis_size("ens")
    strip_start = lax.axis_index("ens") * strip_width
    strip_input = lax.dynamic_slice_in_dim(cond_padded, strip_start, strip_width + 2, 2)
    mean_strip = network_pass(strip_input, reg_weights, strip_pad, lower_each)
    reg_mean = lax.all_gather(mean_strip, "ens", axis=2, tiled=True)
    mean_input = reg_mean.astype(jnp.bfloat16)
    residual_field = sigma_top * member_noise[0]
    for step_index in range(STEPS):
        sigma_now = sigma_top * sigma_ratio**step_index
        sigma_next = sigma_top * sigma_ratio ** (step_index + 1) if step_index + 1 < STEPS else 0.0
        scale_sq = sigma_now**2 + sigma_data**2
        in_gain = 1.0 / scale_sq**0.5
        skip_gain = sigma_data**2 / scale_sq
        out_gain = sigma_now * sigma_data / scale_sq**0.5
        inputs = jnp.concatenate(
            [(in_gain * residual_field).astype(jnp.bfloat16), conditioning, mean_input], axis=0
        )
        inputs_padded = with_halo(inputs, (("tile", 1),), 1)
        inputs_padded = jnp.pad(inputs_padded, ((0, 0), (0, 0), (1, 1)))
        network = network_pass(inputs_padded, dif_weights, feat_pad, lower_each)
        denoised = skip_gain * residual_field + out_gain * network
        residual_field = residual_field + (sigma_next - sigma_now) / sigma_now * (
            residual_field - denoised
        )
    return (reg_mean + residual_field)[None]


def solution(mesh):
    return jax.shard_map(
        shards,
        mesh=mesh,
        in_specs=(
            P(None, "tile", None),
            P("ens", None, "tile", None),
            P(),
            P(),
            P(),
            P(),
            P(),
            P(),
            P(),
            P(),
            P(),
            P(),
            P(),
            P(),
        ),
        out_specs=P("ens", None, "tile", None),
        check_vma=False,
    )
```

profile of v0, /device:TPU:27, one launch (start us, length us, event | category | flops | bytes accessed | tf_op | source)
XLA Modules:
  0.0 311.5 jit_solution(14510241800380738027)
XLA Ops:
  1.0 2.6 collective-permute-start.1
  3.7 5.1 %collective-permute-start = (bf16[12,1,128]{0,2,1:T(8,128)(2,1)S(1)}, bf16[12,1,128]{0,2,1:T(8,128)(2,1)S(1)}, u32[]{:S(2)}, u32[]{:S(2)}) collective-permute-start(bf16[12,1,128]{0,2,1:T(8,128)(2,1)S(1)} %copy.39), channel_id=1, source_target_pairs={{0,1},{1,2},{2,3},{3,4},{4,5},{5,6},{6,7},{7,8},{8,9},{9,10},{10,1... | collective-permute-start | bytes 9224 | tf_op jit(solution)/shard_map/ppermute | solution.py:20
  11.3 3.7 %collective-permute-start.2 = (bf16[8,1,128]{2,1,0:T(2,128)(2,1)S(1)}, bf16[8,1,128]{2,1,0:T(2,128)(2,1)S(1)}, u32[]{:S(2)}, u32[]{:S(2)}) collective-permute-start(bf16[8,1,128]{2,1,0:T(2,128)(2,1)S(1)} %get-tuple-element.45), channel_id=1, source_target_pairs={{0,32},{32,64},{64,96},{96,128},{128,160},{160,192},{192,224},{224... | collective-permute-start | bytes 6152 | tf_op jit(solution)/shard_map/ppermute | solution.py:20
  17.0 4.0 %collective-permute-done.3 = bf16[8,1,128]{2,1,0:T(2,128)(2,1)S(1)} collective-permute-done((bf16[8,1,128]{2,1,0:T(2,128)(2,1)S(1)}, bf16[8,1,128]{2,1,0:T(2,128)(2,1)S(1)}, u32[]{:S(2)}, u32[]{:S(2)}) %collective-permute-start.3) | collective-permute-done | bytes 2080 | tf_op jit(solution)/shard_map/ppermute | solution.py:22
  21.1 8.4 %collective-permute-start.4 = (bf16[1,10,128]{2,1,0:T(8,128)(2,1)S(1)}, bf16[1,10,128]{2,1,0:T(8,128)(2,1)S(1)}, u32[]{:S(2)}, u32[]{:S(2)}) collective-permute-start(bf16[1,10,128]{2,1,0:T(8,128)(2,1)S(1)} %get-tuple-element.29), channel_id=1, source_target_pairs={{0,1},{1,2},{2,3},{3,4},{4,5},{5,6},{6,7},{7,8},{8,9},{9,10},{10,1... | collective-permute-start | bytes 7688 | tf_op jit(solution)/shard_map/ppermute | solution.py:20
  29.5 1.9 collective-permute-start.5
  31.7 4.8 %collective-permute-done.5 = bf16[1,10,128]{2,1,0:T(8,128)(2,1)S(1)} collective-permute-done((bf16[1,10,128]{2,1,0:T(8,128)(2,1)S(1)}, bf16[1,10,128]{2,1,0:T(8,128)(2,1)S(1)}, u32[]{:S(2)}, u32[]{:S(2)}) %collective-permute-start.5) | collective-permute-done | bytes 2592 | tf_op jit(solution)/shard_map/ppermute | solution.py:22
  37.8 4.5 %collective-permute-start.6 = (bf16[4,1,128]{2,1,0:T(2,128)(2,1)S(1)}, bf16[4,1,128]{2,1,0:T(2,128)(2,1)S(1)}, u32[]{:S(2)}, u32[]{:S(2)}) collective-permute-start(bf16[4,1,128]{2,1,0:T(2,128)(2,1)S(1)} %get-tuple-element.57), channel_id=1, source_target_pairs={{0,32},{32,64},{64,96},{96,128},{128,160},{160,192},{192,224},{224... | collective-permute-start | bytes 3080 | tf_op jit(solution)/shard_map/ppermute | solution.py:20
  43.8 4.4 %collective-permute-done.7 = bf16[4,1,128]{2,1,0:T(2,128)(2,1)S(1)} collective-permute-done((bf16[4,1,128]{2,1,0:T(2,128)(2,1)S(1)}, bf16[4,1,128]{2,1,0:T(2,128)(2,1)S(1)}, u32[]{:S(2)}, u32[]{:S(2)}) %collective-permute-start.7) | collective-permute-done | bytes 1056 | tf_op jit(solution)/shard_map/ppermute | solution.py:22
  48.2 4.0 %collective-permute-start.8 = (bf16[1,6,128]{2,1,0:T(8,128)(2,1)S(1)}, bf16[1,6,128]{2,1,0:T(8,128)(2,1)S(1)}, u32[]{:S(2)}, u32[]{:S(2)}) collective-permute-start(bf16[1,6,128]{2,1,0:T(8,128)(2,1)S(1)} %get-tuple-element.53), channel_id=1, source_target_pairs={{0,1},{1,2},{2,3},{3,4},{4,5},{5,6},{6,7},{7,8},{8,9},{9,10},{10,1... | collective-permute-start | bytes 4616 | tf_op jit(solution)/shard_map/ppermute | solution.py:20
  52.2 1.9 collective-permute-start.9
  54.2 4.9 %collective-permute-done.9 = bf16[1,6,128]{2,1,0:T(8,128)(2,1)S(1)} collective-permute-done((bf16[1,6,128]{2,1,0:T(8,128)(2,1)S(1)}, bf16[1,6,128]{2,1,0:T(8,128)(2,1)S(1)}, u32[]{:S(2)}, u32[]{:S(2)}) %collective-permute-start.9) | collective-permute-done | bytes 1568 | tf_op jit(solution)/shard_map/ppermute | solution.py:22
  60.6 3.8 %collective-permute-start.10 = (bf16[4,1,128]{2,1,0:T(2,128)(2,1)S(1)}, bf16[4,1,128]{2,1,0:T(2,128)(2,1)S(1)}, u32[]{:S(2)}, u32[]{:S(2)}) collective-permute-start(bf16[4,1,128]{2,1,0:T(2,128)(2,1)S(1)} %get-tuple-element.55), channel_id=1, source_target_pairs={{0,32},{32,64},{64,96},{96,128},{128,160},{160,192},{192,224},{224... | collective-permute-start | bytes 3080 | tf_op jit(solution)/shard_map/ppermute | solution.py:20
  65.8 4.4 %collective-permute-done.11 = bf16[4,1,128]{2,1,0:T(2,128)(2,1)S(1)} collective-permute-done((bf16[4,1,128]{2,1,0:T(2,128)(2,1)S(1)}, bf16[4,1,128]{2,1,0:T(2,128)(2,1)S(1)}, u32[]{:S(2)}, u32[]{:S(2)}) %collective-permute-start.11) | collective-permute-done | bytes 1056 | tf_op jit(solution)/shard_map/ppermute | solution.py:22
  70.2 4.0 %collective-permute-start.12 = (bf16[1,6,128]{2,1,0:T(8,128)(2,1)S(1)}, bf16[1,6,128]{2,1,0:T(8,128)(2,1)S(1)}, u32[]{:S(2)}, u32[]{:S(2)}) collective-permute-start(bf16[1,6,128]{2,1,0:T(8,128)(2,1)S(1)} %get-tuple-element.49), channel_id=1, source_target_pairs={{0,1},{1,2},{2,3},{3,4},{4,5},{5,6},{6,7},{7,8},{8,9},{9,10},{10,1... | collective-permute-start | bytes 4616 | tf_op jit(solution)/shard_map/ppermute | solution.py:20
  74.2 1.9 collective-permute-start.13
  76.4 4.8 %collective-permute-done.13 = bf16[1,6,128]{2,1,0:T(8,128)(2,1)S(1)} collective-permute-done((bf16[1,6,128]{2,1,0:T(8,128)(2,1)S(1)}, bf16[1,6,128]{2,1,0:T(8,128)(2,1)S(1)}, u32[]{:S(2)}, u32[]{:S(2)}) %collective-permute-start.13) | collective-permute-done | bytes 1568 | tf_op jit(solution)/shard_map/ppermute | solution.py:22
  82.7 4.5 %collective-permute-start.14 = (bf16[8,1,128]{2,1,0:T(2,128)(2,1)S(1)}, bf16[8,1,128]{2,1,0:T(2,128)(2,1)S(1)}, u32[]{:S(2)}, u32[]{:S(2)}) collective-permute-start(bf16[8,1,128]{2,1,0:T(2,128)(2,1)S(1)} %get-tuple-element.43), channel_id=1, source_target_pairs={{0,32},{32,64},{64,96},{96,128},{128,160},{160,192},{192,224},{224... | collective-permute-start | bytes 6152 | tf_op jit(solution)/shard_map/ppermute | solution.py:20
  88.6 4.4 %collective-permute-done.15 = bf16[8,1,128]{2,1,0:T(2,128)(2,1)S(1)} collective-permute-done((bf16[8,1,128]{2,1,0:T(2,128)(2,1)S(1)}, bf16[8,1,128]{2,1,0:T(2,128)(2,1)S(1)}, u32[]{:S(2)}, u32[]{:S(2)}) %collective-permute-start.15) | collective-permute-done | bytes 2080 | tf_op jit(solution)/shard_map/ppermute | solution.py:22
  93.1 4.0 %collective-permute-start.16 = (bf16[1,10,128]{2,1,0:T(8,128)(2,1)S(1)}, bf16[1,10,128]{2,1,0:T(8,128)(2,1)S(1)}, u32[]{:S(2)}, u32[]{:S(2)}) collective-permute-start(bf16[1,10,128]{2,1,0:T(8,128)(2,1)S(1)} %get-tuple-element.37), channel_id=1, source_target_pairs={{0,1},{1,2},{2,3},{3,4},{4,5},{5,6},{6,7},{7,8},{8,9},{9,10},{10,1... | collective-permute-start | bytes 7688 | tf_op jit(solution)/shard_map/ppermute | solution.py:20
  97.1 1.9 collective-permute-start.17
  99.1 5.0 %collective-permute-done.17 = bf16[1,10,128]{2,1,0:T(8,128)(2,1)S(1)} collective-permute-done((bf16[1,10,128]{2,1,0:T(8,128)(2,1)S(1)}, bf16[1,10,128]{2,1,0:T(8,128)(2,1)S(1)}, u32[]{:S(2)}, u32[]{:S(2)}) %collective-permute-start.17) | collective-permute-done | bytes 2592 | tf_op jit(solution)/shard_map/ppermute | solution.py:22
  105.1 3.8 %collective-permute-start.18 = (bf16[8,1,128]{2,1,0:T(2,128)(2,1)S(1)}, bf16[8,1,128]{2,1,0:T(2,128)(2,1)S(1)}, u32[]{:S(2)}, u32[]{:S(2)}) collective-permute-start(bf16[8,1,128]{2,1,0:T(2,128)(2,1)S(1)} %get-tuple-element.41), channel_id=1, source_target_pairs={{0,32},{32,64},{64,96},{96,128},{128,160},{160,192},{192,224},{224... | collective-permute-start | bytes 6152 | tf_op jit(solution)/shard_map/ppermute | solution.py:20
  110.4 4.4 %collective-permute-done.19 = bf16[8,1,128]{2,1,0:T(2,128)(2,1)S(1)} collective-permute-done((bf16[8,1,128]{2,1,0:T(2,128)(2,1)S(1)}, bf16[8,1,128]{2,1,0:T(2,128)(2,1)S(1)}, u32[]{:S(2)}, u32[]{:S(2)}) %collective-permute-start.19) | collective-permute-done | bytes 2080 | tf_op jit(solution)/shard_map/ppermute | solution.py:22
  114.8 4.0 %collective-permute-start.20 = (bf16[1,10,128]{2,1,0:T(8,128)(2,1)S(1)}, bf16[1,10,128]{2,1,0:T(8,128)(2,1)S(1)}, u32[]{:S(2)}, u32[]{:S(2)}) collective-permute-start(bf16[1,10,128]{2,1,0:T(8,128)(2,1)S(1)} %get-tuple-element.33), channel_id=1, source_target_pairs={{0,1},{1,2},{2,3},{3,4},{4,5},{5,6},{6,7},{7,8},{8,9},{9,10},{10,1... | collective-permute-start | bytes 7688 | tf_op jit(solution)/shard_map/ppermute | solution.py:20
  118.8 1.9 collective-permute-start.21
  120.9 4.9 %collective-permute-done.21 = bf16[1,10,128]{2,1,0:T(8,128)(2,1)S(1)} collective-permute-done((bf16[1,10,128]{2,1,0:T(8,128)(2,1)S(1)}, bf16[1,10,128]{2,1,0:T(8,128)(2,1)S(1)}, u32[]{:S(2)}, u32[]{:S(2)}) %collective-permute-start.21) | collective-permute-done | bytes 2592 | tf_op jit(solution)/shard_map/ppermute | solution.py:22
  127.2 35.0 %all_gather.3 = f32[4,8,128]{1,0,2:T(4,128)S(1)} all-gather(f32[4,8,8]{1,0,2:T(4,128)S(1)} %copy.43), channel_id=1, replica_groups=mesh['ens'=16,'tile'=32] {'ens'}, dimensions={2}, use_global_device_ids=true | all-gather | bytes 17408 | tf_op jit(solution)/shard_map/all_gather | solution.py:150
  162.4 9.7 %collective-permute-start.22 = (bf16[20,1,128]{2,0,1:T(8,128)(2,1)S(1)}, bf16[20,1,128]{2,0,1:T(8,128)(2,1)S(1)}, u32[]{:S(2)}, u32[]{:S(2)}) collective-permute-start(bf16[20,1,128]{2,0,1:T(8,128)(2,1)S(1)} %get-tuple-element.27), channel_id=1, source_target_pairs={{0,1},{1,2},{2,3},{3,4},{4,5},{5,6},{6,7},{7,8},{8,9},{9,10},{10,1... | collective-permute-start | bytes 15368 | tf_op jit(solution)/shard_map/ppermute | solution.py:20
  172.1 2.1 collective-permute-start.23
  174.2 5.1 %collective-permute-done.23 = bf16[20,1,128]{2,0,1:T(8,128)(2,1)S(1)} collective-permute-done((bf16[20,1,128]{2,0,1:T(8,128)(2,1)S(1)}, bf16[20,1,128]{2,0,1:T(8,128)(2,1)S(1)}, u32[]{:S(2)}, u32[]{:S(2)}) %collective-permute-start.23) | collective-permute-done | bytes 5152 | tf_op jit(solution)/shard_map/ppermute | solution.py:22
  182.4 1.9 collective-permute-start.24
  184.4 2.4 collective-permute-start.25
  186.8 4.9 %collective-permute-done.25 = bf16[1,128,128]{2,1,0:T(8,128)(2,1)S(1)} collective-permute-done((bf16[1,128,128]{2,1,0:T(8,128)(2,1)S(1)}, bf16[1,128,128]{2,1,0:T(8,128)(2,1)S(1)}, u32[]{:S(2)}, u32[]{:S(2)}) %collective-permute-start.25) | collective-permute-done | bytes 32800 | tf_op jit(solution)/shard_map/ppermute | solution.py:22
  195.1 1.9 collective-permute-start.26
  197.0 2.4 collective-permute-start.27
  199.5 4.7 %collective-permute-done.27 = bf16[1,64,128]{2,1,0:T(8,128)(2,1)S(1)} collective-permute-done((bf16[1,64,128]{2,1,0:T(8,128)(2,1)S(1)}, bf16[1,64,128]{2,1,0:T(8,128)(2,1)S(1)}, u32[]{:S(2)}, u32[]{:S(2)}) %collective-permute-start.27) | collective-permute-done | bytes 16416 | tf_op jit(solution)/shard_map/ppermute | solution.py:22
  206.8 1.9 collective-permute-start.28
  208.8 2.4 collective-permute-start.29
  211.3 4.6 %collective-permute-done.29 = bf16[1,64,128]{2,1,0:T(8,128)(2,1)S(1)} collective-permute-done((bf16[1,64,128]{2,1,0:T(8,128)(2,1)S(1)}, bf16[1,64,128]{2,1,0:T(8,128)(2,1)S(1)}, u32[]{:S(2)}, u32[]{:S(2)}) %collective-permute-start.29) | collective-permute-done | bytes 16416 | tf_op jit(solution)/shard_map/ppermute | solution.py:22
  218.6 1.9 collective-permute-start.30
  220.5 2.5 collective-permute-start.31
  223.1 4.9 %collective-permute-done.31 = bf16[1,128,128]{2,1,0:T(8,128)(2,1)S(1)} collective-permute-done((bf16[1,128,128]{2,1,0:T(8,128)(2,1)S(1)}, bf16[1,128,128]{2,1,0:T(8,128)(2,1)S(1)}, u32[]{:S(2)}, u32[]{:S(2)}) %collective-permute-start.31) | collective-permute-done | bytes 32800 | tf_op jit(solution)/shard_map/ppermute | solution.py:22
  230.2 1.9 collective-permute-start.32
  232.1 2.4 collective-permute-start.33
  234.5 4.9 %collective-permute-done.33 = bf16[1,128,128]{2,1,0:T(8,128)(2,1)S(1)} collective-permute-done((bf16[1,128,128]{2,1,0:T(8,128)(2,1)S(1)}, bf16[1,128,128]{2,1,0:T(8,128)(2,1)S(1)}, u32[]{:S(2)}, u32[]{:S(2)}) %collective-permute-start.33) | collective-permute-done | bytes 32800 | tf_op jit(solution)/shard_map/ppermute | solution.py:22
  241.3 1.9 collective-permute-start.34
  243.2 2.6 collective-permute-start.35
  245.8 4.5 %collective-permute-done.35 = bf16[20,1,128]{2,0,1:T(8,128)(2,1)S(1)} collective-permute-done((bf16[20,1,128]{2,0,1:T(8,128)(2,1)S(1)}, bf16[20,1,128]{2,0,1:T(8,128)(2,1)S(1)}, u32[]{:S(2)}, u32[]{:S(2)}) %collective-permute-start.35) | collective-permute-done | bytes 5152 | tf_op jit(solution)/shard_map/ppermute | solution.py:22
  253.4 1.9 collective-permute-start.36
  255.3 2.4 collective-permute-start.37
  257.7 4.9 %collective-permute-done.37 = bf16[1,128,128]{2,1,0:T(8,128)(2,1)S(1)} collective-permute-done((bf16[1,128,128]{2,1,0:T(8,128)(2,1)S(1)}, bf16[1,128,128]{2,1,0:T(8,128)(2,1)S(1)}, u32[]{:S(2)}, u32[]{:S(2)}) %collective-permute-start.37) | collective-permute-done | bytes 32800 | tf_op jit(solution)/shard_map/ppermute | solution.py:22
  265.8 1.9 collective-permute-start.38
  267.7 2.4 collective-permute-start.39
  270.1 4.7 %collective-permute-done.39 = bf16[1,64,128]{2,1,0:T(8,128)(2,1)S(1)} collective-permute-done((bf16[1,64,128]{2,1,0:T(8,128)(2,1)S(1)}, bf16[1,64,128]{2,1,0:T(8,128)(2,1)S(1)}, u32[]{:S(2)}, u32[]{:S(2)}) %collective-permute-start.39) | collective-permute-done | bytes 16416 | tf_op jit(solution)/shard_map/ppermute | solution.py:22
  276.6 1.9 collective-permute-start.40
  278.6 2.4 collective-permute-start.41
  281.1 4.6 %collective-permute-done.41 = bf16[1,64,128]{2,1,0:T(8,128)(2,1)S(1)} collective-permute-done((bf16[1,64,128]{2,1,0:T(8,128)(2,1)S(1)}, bf16[1,64,128]{2,1,0:T(8,128)(2,1)S(1)}, u32[]{:S(2)}, u32[]{:S(2)}) %collective-permute-start.41) | collective-permute-done | bytes 16416 | tf_op jit(solution)/shard_map/ppermute | solution.py:22
  288.4 1.9 collective-permute-start.42
  290.3 2.4 collective-permute-start.43
  292.7 4.9 %collective-permute-done.43 = bf16[1,128,128]{2,1,0:T(8,128)(2,1)S(1)} collective-permute-done((bf16[1,128,128]{2,1,0:T(8,128)(2,1)S(1)}, bf16[1,128,128]{2,1,0:T(8,128)(2,1)S(1)}, u32[]{:S(2)}, u32[]{:S(2)}) %collective-permute-start.43) | collective-permute-done | bytes 32800 | tf_op jit(solution)/shard_map/ppermute | solution.py:22
  299.8 1.9 collective-permute-start.44
  301.8 2.4 collective-permute-start.45
  304.2 4.9 %collective-permute-done.45 = bf16[1,128,128]{2,1,0:T(8,128)(2,1)S(1)} collective-permute-done((bf16[1,128,128]{2,1,0:T(8,128)(2,1)S(1)}, bf16[1,128,128]{2,1,0:T(8,128)(2,1)S(1)}, u32[]{:S(2)}, u32[]{:S(2)}) %collective-permute-start.45) | collective-permute-done | bytes 32800 | tf_op jit(solution)/shard_map/ppermute | solution.py:22
  (334 shorter events, 49.1 us)
Async XLA Ops:
  1.0 8.1 %collective-permute-start.1 = (bf16[12,1,128]{0,2,1:T(8,128)(2,1)S(1)}, bf16[12,1,128]{0,2,1:T(8,128)(2,1)S(1)}, u32[]{:S(2)}, u32[]{:S(2)}) collective-permute-start(bf16[12,1,128]{0,2,1:T(8,128)(2,1)S(1)} %copy.40), channel_id=1, source_target_pairs={{1,0},{2,1},{3,2},{4,3},{5,4},{6,5},{7,6},{8,7},{9,8},{10,9},{11,1... | collective-permute-start | bytes 9224 | tf_op jit(solution)/shard_map/ppermute | solution.py:22
  3.5 5.2 %copy-start.11 = (f32[1,4,8,128]{3,2,1,0:T(8,128)S(1)}, f32[1,4,8,128]{3,2,1,0:T(8,128)}, u32[]{:S(2)}) copy-start(f32[1,4,8,128]{3,2,1,0:T(8,128)} %param.15) | copy-start | bytes 49156
  3.6 5.3 %copy-start.9 = (bf16[12,8,128]{2,1,0:T(8,128)(2,1)S(1)}, bf16[12,8,128]{2,1,0:T(8,128)(2,1)}, u32[]{:S(2)}) copy-start(bf16[12,8,128]{2,1,0:T(8,128)(2,1)} %param.14) | copy-start | bytes 73732
  3.7 6.1 %collective-permute-start = (bf16[12,1,128]{0,2,1:T(8,128)(2,1)S(1)}, bf16[12,1,128]{0,2,1:T(8,128)(2,1)S(1)}, u32[]{:S(2)}, u32[]{:S(2)}) collective-permute-start(bf16[12,1,128]{0,2,1:T(8,128)(2,1)S(1)} %copy.39), channel_id=1, source_target_pairs={{0,1},{1,2},{2,3},{3,4},{4,5},{5,6},{6,7},{7,8},{8,9},{9,10},{10,1... | collective-permute-start | bytes 9224 | tf_op jit(solution)/shard_map/ppermute | solution.py:20
  9.1 0.8 copy-start.10
  10.4 6.0 %copy-start.6 = (bf16[3,3,128,128]{3,2,1,0:T(8,128)(2,1)S(1)}, bf16[3,3,128,128]{3,2,1,0:T(8,128)(2,1)}, u32[]{:S(2)}) copy-start(bf16[3,3,128,128]{3,2,1,0:T(8,128)(2,1)} %param.17) | copy-start | bytes 884740
  11.3 5.6 %collective-permute-start.2 = (bf16[8,1,128]{2,1,0:T(2,128)(2,1)S(1)}, bf16[8,1,128]{2,1,0:T(2,128)(2,1)S(1)}, u32[]{:S(2)}, u32[]{:S(2)}) collective-permute-start(bf16[8,1,128]{2,1,0:T(2,128)(2,1)S(1)} %get-tuple-element.45), channel_id=1, source_target_pairs={{0,32},{32,64},{64,96},{96,128},{128,160},{160,192},{192,224},{224... | collective-permute-start | bytes 6152 | tf_op jit(solution)/shard_map/ppermute | solution.py:20
  15.1 5.9 %collective-permute-start.3 = (bf16[8,1,128]{2,1,0:T(2,128)(2,1)S(1)}, bf16[8,1,128]{2,1,0:T(2,128)(2,1)S(1)}, u32[]{:S(2)}, u32[]{:S(2)}) collective-permute-start(bf16[8,1,128]{2,1,0:T(2,128)(2,1)S(1)} %get-tuple-element.46), channel_id=1, source_target_pairs={{32,0},{64,32},{96,64},{128,96},{160,128},{192,160},{224,192},{256... | collective-permute-start | bytes 6152 | tf_op jit(solution)/shard_map/ppermute | solution.py:22
  21.0 22.6 %copy-start.5 = (bf16[3,3,128,128]{3,2,1,0:T(8,128)(2,1)S(1)}, bf16[3,3,128,128]{3,2,1,0:T(8,128)(2,1)}, u32[]{:S(2)}) copy-start(bf16[3,3,128,128]{3,2,1,0:T(8,128)(2,1)} %param.18) | copy-start | bytes 884740
  21.1 10.6 %collective-permute-start.4 = (bf16[1,10,128]{2,1,0:T(8,128)(2,1)S(1)}, bf16[1,10,128]{2,1,0:T(8,128)(2,1)S(1)}, u32[]{:S(2)}, u32[]{:S(2)}) collective-permute-start(bf16[1,10,128]{2,1,0:T(8,128)(2,1)S(1)} %get-tuple-element.29), channel_id=1, source_target_pairs={{0,1},{1,2},{2,3},{3,4},{4,5},{5,6},{6,7},{7,8},{8,9},{9,10},{10,1... | collective-permute-start | bytes 7688 | tf_op jit(solution)/shard_map/ppermute | solution.py:20
  29.5 7.0 %collective-permute-start.5 = (bf16[1,10,128]{2,1,0:T(8,128)(2,1)S(1)}, bf16[1,10,128]{2,1,0:T(8,128)(2,1)S(1)}, u32[]{:S(2)}, u32[]{:S(2)}) collective-permute-start(bf16[1,10,128]{2,1,0:T(8,128)(2,1)S(1)} %get-tuple-element.30), channel_id=1, source_target_pairs={{1,0},{2,1},{3,2},{4,3},{5,4},{6,5},{7,6},{8,7},{9,8},{10,9},{11,1... | collective-permute-start | bytes 7688 | tf_op jit(solution)/shard_map/ppermute | solution.py:22
  36.6 23.6 %copy-start.4 = (bf16[4,4,128,128]{3,2,1,0:T(8,128)(2,1)S(1)}, bf16[4,4,128,128]{3,2,1,0:T(8,128)(2,1)}, u32[]{:S(2)}) copy-start(bf16[4,4,128,128]{3,2,1,0:T(8,128)(2,1)} %param.19) | copy-start | bytes 1572868
  37.8 6.0 %collective-permute-start.6 = (bf16[4,1,128]{2,1,0:T(2,128)(2,1)S(1)}, bf16[4,1,128]{2,1,0:T(2,128)(2,1)S(1)}, u32[]{:S(2)}, u32[]{:S(2)}) collective-permute-start(bf16[4,1,128]{2,1,0:T(2,128)(2,1)S(1)} %get-tuple-element.57), channel_id=1, source_target_pairs={{0,32},{32,64},{64,96},{96,128},{128,160},{160,192},{192,224},{224... | collective-permute-start | bytes 3080 | tf_op jit(solution)/shard_map/ppermute | solution.py:20
  42.3 5.8 %collective-permute-start.7 = (bf16[4,1,128]{2,1,0:T(2,128)(2,1)S(1)}, bf16[4,1,128]{2,1,0:T(2,128)(2,1)S(1)}, u32[]{:S(2)}, u32[]{:S(2)}) collective-permute-start(bf16[4,1,128]{2,1,0:T(2,128)(2,1)S(1)} %get-tuple-element.58), channel_id=1, source_target_pairs={{32,0},{64,32},{96,64},{128,96},{160,128},{192,160},{224,192},{256... | collective-permute-start | bytes 3080 | tf_op jit(solution)/shard_map/ppermute | solution.py:22
  48.2 6.1 %collective-permute-start.8 = (bf16[1,6,128]{2,1,0:T(8,128)(2,1)S(1)}, bf16[1,6,128]{2,1,0:T(8,128)(2,1)S(1)}, u32[]{:S(2)}, u32[]{:S(2)}) collective-permute-start(bf16[1,6,128]{2,1,0:T(8,128)(2,1)S(1)} %get-tuple-element.53), channel_id=1, source_target_pairs={{0,1},{1,2},{2,3},{3,4},{4,5},{5,6},{6,7},{7,8},{8,9},{9,10},{10,1... | collective-permute-start | bytes 4616 | tf_op jit(solution)/shard_map/ppermute | solution.py:20
  52.2 7.0 %collective-permute-start.9 = (bf16[1,6,128]{2,1,0:T(8,128)(2,1)S(1)}, bf16[1,6,128]{2,1,0:T(8,128)(2,1)S(1)}, u32[]{:S(2)}, u32[]{:S(2)}) collective-permute-start(bf16[1,6,128]{2,1,0:T(8,128)(2,1)S(1)} %get-tuple-element.54), channel_id=1, source_target_pairs={{1,0},{2,1},{3,2},{4,3},{5,4},{6,5},{7,6},{8,7},{9,8},{10,9},{11,1... | collective-permute-start | bytes 4616 | tf_op jit(solution)/shard_map/ppermute | solution.py:22
  60.6 5.2 %collective-permute-start.10 = (bf16[4,1,128]{2,1,0:T(2,128)(2,1)S(1)}, bf16[4,1,128]{2,1,0:T(2,128)(2,1)S(1)}, u32[]{:S(2)}, u32[]{:S(2)}) collective-permute-start(bf16[4,1,128]{2,1,0:T(2,128)(2,1)S(1)} %get-tuple-element.55), channel_id=1, source_target_pairs={{0,32},{32,64},{64,96},{96,128},{128,160},{160,192},{192,224},{224... | collective-permute-start | bytes 3080 | tf_op jit(solution)/shard_map/ppermute | solution.py:20
  64.3 5.8 %collective-permute-start.11 = (bf16[4,1,128]{2,1,0:T(2,128)(2,1)S(1)}, bf16[4,1,128]{2,1,0:T(2,128)(2,1)S(1)}, u32[]{:S(2)}, u32[]{:S(2)}) collective-permute-start(bf16[4,1,128]{2,1,0:T(2,128)(2,1)S(1)} %get-tuple-element.56), channel_id=1, source_target_pairs={{32,0},{64,32},{96,64},{128,96},{160,128},{192,160},{224,192},{256... | collective-permute-start | bytes 3080 | tf_op jit(solution)/shard_map/ppermute | solution.py:22
  70.2 6.2 %collective-permute-start.12 = (bf16[1,6,128]{2,1,0:T(8,128)(2,1)S(1)}, bf16[1,6,128]{2,1,0:T(8,128)(2,1)S(1)}, u32[]{:S(2)}, u32[]{:S(2)}) collective-permute-start(bf16[1,6,128]{2,1,0:T(8,128)(2,1)S(1)} %get-tuple-element.49), channel_id=1, source_target_pairs={{0,1},{1,2},{2,3},{3,4},{4,5},{5,6},{6,7},{7,8},{8,9},{9,10},{10,1... | collective-permute-start | bytes 4616 | tf_op jit(solution)/shard_map/ppermute | solution.py:20
  74.2 7.0 %collective-permute-start.13 = (bf16[1,6,128]{2,1,0:T(8,128)(2,1)S(1)}, bf16[1,6,128]{2,1,0:T(8,128)(2,1)S(1)}, u32[]{:S(2)}, u32[]{:S(2)}) collective-permute-start(bf16[1,6,128]{2,1,0:T(8,128)(2,1)S(1)} %get-tuple-element.50), channel_id=1, source_target_pairs={{1,0},{2,1},{3,2},{4,3},{5,4},{6,5},{7,6},{8,7},{9,8},{10,9},{11,1... | collective-permute-start | bytes 4616 | tf_op jit(solution)/shard_map/ppermute | solution.py:22
  81.9 6.6 %copy-start.7 = (bf16[3,3,128,128]{3,2,1,0:T(8,128)(2,1)S(1)}, bf16[3,3,128,128]{3,2,1,0:T(8,128)(2,1)}, u32[]{:S(2)}) copy-start(bf16[3,3,128,128]{3,2,1,0:T(8,128)(2,1)} %param.20) | copy-start | bytes 884740
  82.7 6.0 %collective-permute-start.14 = (bf16[8,1,128]{2,1,0:T(2,128)(2,1)S(1)}, bf16[8,1,128]{2,1,0:T(2,128)(2,1)S(1)}, u32[]{:S(2)}, u32[]{:S(2)}) collective-permute-start(bf16[8,1,128]{2,1,0:T(2,128)(2,1)S(1)} %get-tuple-element.43), channel_id=1, source_target_pairs={{0,32},{32,64},{64,96},{96,128},{128,160},{160,192},{192,224},{224... | collective-permute-start | bytes 6152 | tf_op jit(solution)/shard_map/ppermute | solution.py:20
  87.2 5.9 %collective-permute-start.15 = (bf16[8,1,128]{2,1,0:T(2,128)(2,1)S(1)}, bf16[8,1,128]{2,1,0:T(2,128)(2,1)S(1)}, u32[]{:S(2)}, u32[]{:S(2)}) collective-permute-start(bf16[8,1,128]{2,1,0:T(2,128)(2,1)S(1)} %get-tuple-element.44), channel_id=1, source_target_pairs={{32,0},{64,32},{96,64},{128,96},{160,128},{192,160},{224,192},{256... | collective-permute-start | bytes 6152 | tf_op jit(solution)/shard_map/ppermute | solution.py:22
  93.1 6.1 %collective-permute-start.16 = (bf16[1,10,128]{2,1,0:T(8,128)(2,1)S(1)}, bf16[1,10,128]{2,1,0:T(8,128)(2,1)S(1)}, u32[]{:S(2)}, u32[]{:S(2)}) collective-permute-start(bf16[1,10,128]{2,1,0:T(8,128)(2,1)S(1)} %get-tuple-element.37), channel_id=1, source_target_pairs={{0,1},{1,2},{2,3},{3,4},{4,5},{5,6},{6,7},{7,8},{8,9},{9,10},{10,1... | collective-permute-start | bytes 7688 | tf_op jit(solution)/shard_map/ppermute | solution.py:20
  97.1 7.0 %collective-permute-start.17 = (bf16[1,10,128]{2,1,0:T(8,128)(2,1)S(1)}, bf16[1,10,128]{2,1,0:T(8,128)(2,1)S(1)}, u32[]{:S(2)}, u32[]{:S(2)}) collective-permute-start(bf16[1,10,128]{2,1,0:T(8,128)(2,1)S(1)} %get-tuple-element.38), channel_id=1, source_target_pairs={{1,0},{2,1},{3,2},{4,3},{5,4},{6,5},{7,6},{8,7},{9,8},{10,9},{11,1... | collective-permute-start | bytes 7688 | tf_op jit(solution)/shard_map/ppermute | solution.py:22
  105.1 5.1 %copy-start.12 = (bf16[3,3,4,128]{3,2,1,0:T(4,128)(2,1)S(1)}, bf16[3,3,4,128]{3,2,1,0:T(4,128)(2,1)}, u32[]{:S(2)}) copy-start(bf16[3,3,4,128]{3,2,1,0:T(4,128)(2,1)} %param.21) | copy-start | bytes 27652
  105.1 5.2 %collective-permute-start.18 = (bf16[8,1,128]{2,1,0:T(2,128)(2,1)S(1)}, bf16[8,1,128]{2,1,0:T(2,128)(2,1)S(1)}, u32[]{:S(2)}, u32[]{:S(2)}) collective-permute-start(bf16[8,1,128]{2,1,0:T(2,128)(2,1)S(1)} %get-tuple-element.41), channel_id=1, source_target_pairs={{0,32},{32,64},{64,96},{96,128},{128,160},{160,192},{192,224},{224... | collective-permute-start | bytes 6152 | tf_op jit(solution)/shard_map/ppermute | solution.py:20
  108.9 5.9 %collective-permute-start.19 = (bf16[8,1,128]{2,1,0:T(2,128)(2,1)S(1)}, bf16[8,1,128]{2,1,0:T(2,128)(2,1)S(1)}, u32[]{:S(2)}, u32[]{:S(2)}) collective-permute-start(bf16[8,1,128]{2,1,0:T(2,128)(2,1)S(1)} %get-tuple-element.42), channel_id=1, source_target_pairs={{32,0},{64,32},{96,64},{128,96},{160,128},{192,160},{224,192},{256... | collective-permute-start | bytes 6152 | tf_op jit(solution)/shard_map/ppermute | solution.py:22
  114.8 6.1 %collective-permute-start.20 = (bf16[1,10,128]{2,1,0:T(8,128)(2,1)S(1)}, bf16[1,10,128]{2,1,0:T(8,128)(2,1)S(1)}, u32[]{:S(2)}, u32[]{:S(2)}) collective-permute-start(bf16[1,10,128]{2,1,0:T(8,128)(2,1)S(1)} %get-tuple-element.33), channel_id=1, source_target_pairs={{0,1},{1,2},{2,3},{3,4},{4,5},{5,6},{6,7},{7,8},{8,9},{9,10},{10,1... | collective-permute-start | bytes 7688 | tf_op jit(solution)/shard_map/ppermute | solution.py:20
  118.8 7.0 %collective-permute-start.21 = (bf16[1,10,128]{2,1,0:T(8,128)(2,1)S(1)}, bf16[1,10,128]{2,1,0:T(8,128)(2,1)S(1)}, u32[]{:S(2)}, u32[]{:S(2)}) collective-permute-start(bf16[1,10,128]{2,1,0:T(8,128)(2,1)S(1)} %get-tuple-element.34), channel_id=1, source_target_pairs={{1,0},{2,1},{3,2},{4,3},{5,4},{6,5},{7,6},{8,7},{9,8},{10,9},{11,1... | collective-permute-start | bytes 7688 | tf_op jit(solution)/shard_map/ppermute | solution.py:22
  162.4 11.8 %collective-permute-start.22 = (bf16[20,1,128]{2,0,1:T(8,128)(2,1)S(1)}, bf16[20,1,128]{2,0,1:T(8,128)(2,1)S(1)}, u32[]{:S(2)}, u32[]{:S(2)}) collective-permute-start(bf16[20,1,128]{2,0,1:T(8,128)(2,1)S(1)} %get-tuple-element.27), channel_id=1, source_target_pairs={{0,1},{1,2},{2,3},{3,4},{4,5},{5,6},{6,7},{7,8},{8,9},{9,10},{10,1... | collective-permute-start | bytes 15368 | tf_op jit(solution)/shard_map/ppermute | solution.py:20
  172.1 7.2 %copy-start.8 = (bf16[3,3,20,128]{3,2,1,0:T(8,128)(2,1)S(1)}, bf16[3,3,20,128]{3,2,1,0:T(8,128)(2,1)}, u32[]{:S(2)}) copy-start(bf16[3,3,20,128]{3,2,1,0:T(8,128)(2,1)} %param.22) | copy-start | bytes 138244
  172.1 7.2 %collective-permute-start.23 = (bf16[20,1,128]{2,0,1:T(8,128)(2,1)S(1)}, bf16[20,1,128]{2,0,1:T(8,128)(2,1)S(1)}, u32[]{:S(2)}, u32[]{:S(2)}) collective-permute-start(bf16[20,1,128]{2,0,1:T(8,128)(2,1)S(1)} %get-tuple-element.28), channel_id=1, source_target_pairs={{1,0},{2,1},{3,2},{4,3},{5,4},{6,5},{7,6},{8,7},{9,8},{10,9},{11,1... | collective-permute-start | bytes 15368 | tf_op jit(solution)/shard_map/ppermute | solution.py:22
  182.4 4.3 %collective-permute-start.24 = (bf16[1,128,128]{2,1,0:T(8,128)(2,1)S(1)}, bf16[1,128,128]{2,1,0:T(8,128)(2,1)S(1)}, u32[]{:S(2)}, u32[]{:S(2)}) collective-permute-start(bf16[1,128,128]{2,1,0:T(8,128)(2,1)S(1)} %get-tuple-element.15), channel_id=1, source_target_pairs={{0,1},{1,2},{2,3},{3,4},{4,5},{5,6},{6,7},{7,8},{8,9},{9,10},{10,1... | collective-permute-start | bytes 98312 | tf_op jit(solution)/shard_map/ppermute | solution.py:20
  184.4 7.3 %collective-permute-start.25 = (bf16[1,128,128]{2,1,0:T(8,128)(2,1)S(1)}, bf16[1,128,128]{2,1,0:T(8,128)(2,1)S(1)}, u32[]{:S(2)}, u32[]{:S(2)}) collective-permute-start(bf16[1,128,128]{2,1,0:T(8,128)(2,1)S(1)} %get-tuple-element.16), channel_id=1, source_target_pairs={{1,0},{2,1},{3,2},{4,3},{5,4},{6,5},{7,6},{8,7},{9,8},{10,9},{11,1... | collective-permute-start | bytes 98312 | tf_op jit(solution)/shard_map/ppermute | solution.py:22
  192.7 1.0 copy-start.2
  194.9 9.3 %copy-start.1 = (bf16[3,3,128,128]{3,2,1,0:T(8,128)(2,1)S(1)}, bf16[3,3,128,128]{3,2,1,0:T(8,128)(2,1)}, u32[]{:S(2)}) copy-start(bf16[3,3,128,128]{3,2,1,0:T(8,128)(2,1)} %param.24) | copy-start | bytes 884740
  195.1 4.3 %collective-permute-start.26 = (bf16[1,64,128]{2,1,0:T(8,128)(2,1)S(1)}, bf16[1,64,128]{2,1,0:T(8,128)(2,1)S(1)}, u32[]{:S(2)}, u32[]{:S(2)}) collective-permute-start(bf16[1,64,128]{2,1,0:T(8,128)(2,1)S(1)} %get-tuple-element.23), channel_id=1, source_target_pairs={{0,1},{1,2},{2,3},{3,4},{4,5},{5,6},{6,7},{7,8},{8,9},{9,10},{10,1... | collective-permute-start | bytes 49160 | tf_op jit(solution)/shard_map/ppermute | solution.py:20
  197.0 7.2 %collective-permute-start.27 = (bf16[1,64,128]{2,1,0:T(8,128)(2,1)S(1)}, bf16[1,64,128]{2,1,0:T(8,128)(2,1)S(1)}, u32[]{:S(2)}, u32[]{:S(2)}) collective-permute-start(bf16[1,64,128]{2,1,0:T(8,128)(2,1)S(1)} %get-tuple-element.24), channel_id=1, source_target_pairs={{1,0},{2,1},{3,2},{4,3},{5,4},{6,5},{7,6},{8,7},{9,8},{10,9},{11,1... | collective-permute-start | bytes 49160 | tf_op jit(solution)/shard_map/ppermute | solution.py:22
  205.5 1.0 copy-start
  206.8 4.5 %collective-permute-start.28 = (bf16[1,64,128]{2,1,0:T(8,128)(2,1)S(1)}, bf16[1,64,128]{2,1,0:T(8,128)(2,1)S(1)}, u32[]{:S(2)}, u32[]{:S(2)}) collective-permute-start(bf16[1,64,128]{2,1,0:T(8,128)(2,1)S(1)} %get-tuple-element.21), channel_id=1, source_target_pairs={{0,1},{1,2},{2,3},{3,4},{4,5},{5,6},{6,7},{7,8},{8,9},{9,10},{10,1... | collective-permute-start | bytes 49160 | tf_op jit(solution)/shard_map/ppermute | solution.py:20
  208.8 7.2 %collective-permute-start.29 = (bf16[1,64,128]{2,1,0:T(8,128)(2,1)S(1)}, bf16[1,64,128]{2,1,0:T(8,128)(2,1)S(1)}, u32[]{:S(2)}, u32[]{:S(2)}) collective-permute-start(bf16[1,64,128]{2,1,0:T(8,128)(2,1)S(1)} %get-tuple-element.22), channel_id=1, source_target_pairs={{1,0},{2,1},{3,2},{4,3},{5,4},{6,5},{7,6},{8,7},{9,8},{10,9},{11,1... | collective-permute-start | bytes 49160 | tf_op jit(solution)/shard_map/ppermute | solution.py:22
  218.6 4.5 %collective-permute-start.30 = (bf16[1,128,128]{2,1,0:T(8,128)(2,1)S(1)}, bf16[1,128,128]{2,1,0:T(8,128)(2,1)S(1)}, u32[]{:S(2)}, u32[]{:S(2)}) collective-permute-start(bf16[1,128,128]{2,1,0:T(8,128)(2,1)S(1)} %get-tuple-element.13), channel_id=1, source_target_pairs={{0,1},{1,2},{2,3},{3,4},{4,5},{5,6},{6,7},{7,8},{8,9},{9,10},{10,1... | collective-permute-start | bytes 98312 | tf_op jit(solution)/shard_map/ppermute | solution.py:20
  220.5 7.6 %copy-start.3 = (bf16[3,3,128,128]{3,2,1,0:T(8,128)(2,1)S(1)}, bf16[3,3,128,128]{3,2,1,0:T(8,128)(2,1)}, u32[]{:S(2)}) copy-start(bf16[3,3,128,128]{3,2,1,0:T(8,128)(2,1)} %param.26) | copy-start | bytes 884740
  220.5 7.5 %collective-permute-start.31 = (bf16[1,128,128]{2,1,0:T(8,128)(2,1)S(1)}, bf16[1,128,128]{2,1,0:T(8,128)(2,1)S(1)}, u32[]{:S(2)}, u32[]{:S(2)}) collective-permute-start(bf16[1,128,128]{2,1,0:T(8,128)(2,1)S(1)} %get-tuple-element.14), channel_id=1, source_target_pairs={{1,0},{2,1},{3,2},{4,3},{5,4},{6,5},{7,6},{8,7},{9,8},{10,9},{11,1... | collective-permute-start | bytes 98312 | tf_op jit(solution)/shard_map/ppermute | solution.py:22
  230.2 4.4 %collective-permute-start.32 = (bf16[1,128,128]{2,1,0:T(8,128)(2,1)S(1)}, bf16[1,128,128]{2,1,0:T(8,128)(2,1)S(1)}, u32[]{:S(2)}, u32[]{:S(2)}) collective-permute-start(bf16[1,128,128]{2,1,0:T(8,128)(2,1)S(1)} %get-tuple-element.11), channel_id=1, source_target_pairs={{0,1},{1,2},{2,3},{3,4},{4,5},{5,6},{6,7},{7,8},{8,9},{9,10},{10,1... | collective-permute-start | bytes 98312 | tf_op jit(solution)/shard_map/ppermute | solution.py:20
  232.1 7.5 %copy-start.13 = (bf16[3,3,4,128]{3,2,1,0:T(4,128)(2,1)S(1)}, bf16[3,3,4,128]{3,2,1,0:T(4,128)(2,1)}, u32[]{:S(2)}) copy-start(bf16[3,3,4,128]{3,2,1,0:T(4,128)(2,1)} %param.27) | copy-start | bytes 27652
  232.1 7.3 %collective-permute-start.33 = (bf16[1,128,128]{2,1,0:T(8,128)(2,1)S(1)}, bf16[1,128,128]{2,1,0:T(8,128)(2,1)S(1)}, u32[]{:S(2)}, u32[]{:S(2)}) collective-permute-start(bf16[1,128,128]{2,1,0:T(8,128)(2,1)S(1)} %get-tuple-element.12), channel_id=1, source_target_pairs={{1,0},{2,1},{3,2},{4,3},{5,4},{6,5},{7,6},{8,7},{9,8},{10,9},{11,1... | collective-permute-start | bytes 98312 | tf_op jit(solution)/shard_map/ppermute | solution.py:22
  241.3 4.5 %collective-permute-start.34 = (bf16[20,1,128]{2,0,1:T(8,128)(2,1)S(1)}, bf16[20,1,128]{2,0,1:T(8,128)(2,1)S(1)}, u32[]{:S(2)}, u32[]{:S(2)}) collective-permute-start(bf16[20,1,128]{2,0,1:T(8,128)(2,1)S(1)} %get-tuple-element.25), channel_id=1, source_target_pairs={{0,1},{1,2},{2,3},{3,4},{4,5},{5,6},{6,7},{7,8},{8,9},{9,10},{10,1... | collective-permute-start | bytes 15368 | tf_op jit(solution)/shard_map/ppermute | solution.py:20
  243.2 7.1 %collective-permute-start.35 = (bf16[20,1,128]{2,0,1:T(8,128)(2,1)S(1)}, bf16[20,1,128]{2,0,1:T(8,128)(2,1)S(1)}, u32[]{:S(2)}, u32[]{:S(2)}) collective-permute-start(bf16[20,1,128]{2,0,1:T(8,128)(2,1)S(1)} %get-tuple-element.26), channel_id=1, source_target_pairs={{1,0},{2,1},{3,2},{4,3},{5,4},{6,5},{7,6},{8,7},{9,8},{10,9},{11,1... | collective-permute-start | bytes 15368 | tf_op jit(solution)/shard_map/ppermute | solution.py:22
  253.4 4.3 %collective-permute-start.36 = (bf16[1,128,128]{2,1,0:T(8,128)(2,1)S(1)}, bf16[1,128,128]{2,1,0:T(8,128)(2,1)S(1)}, u32[]{:S(2)}, u32[]{:S(2)}) collective-permute-start(bf16[1,128,128]{2,1,0:T(8,128)(2,1)S(1)} %get-tuple-element.9), channel_id=1, source_target_pairs={{0,1},{1,2},{2,3},{3,4},{4,5},{5,6},{6,7},{7,8},{8,9},{9,10},{10,1... | collective-permute-start | bytes 98312 | tf_op jit(solution)/shard_map/ppermute | solution.py:20
  255.3 7.3 %collective-permute-start.37 = (bf16[1,128,128]{2,1,0:T(8,128)(2,1)S(1)}, bf16[1,128,128]{2,1,0:T(8,128)(2,1)S(1)}, u32[]{:S(2)}, u32[]{:S(2)}) collective-permute-start(bf16[1,128,128]{2,1,0:T(8,128)(2,1)S(1)} %get-tuple-element.10), channel_id=1, source_target_pairs={{1,0},{2,1},{3,2},{4,3},{5,4},{6,5},{7,6},{8,7},{9,8},{10,9},{11,1... | collective-permute-start | bytes 98312 | tf_op jit(solution)/shard_map/ppermute | solution.py:22
  265.8 4.3 %collective-permute-start.38 = (bf16[1,64,128]{2,1,0:T(8,128)(2,1)S(1)}, bf16[1,64,128]{2,1,0:T(8,128)(2,1)S(1)}, u32[]{:S(2)}, u32[]{:S(2)}) collective-permute-start(bf16[1,64,128]{2,1,0:T(8,128)(2,1)S(1)} %get-tuple-element.19), channel_id=1, source_target_pairs={{0,1},{1,2},{2,3},{3,4},{4,5},{5,6},{6,7},{7,8},{8,9},{9,10},{10,1... | collective-permute-start | bytes 49160 | tf_op jit(solution)/shard_map/ppermute | solution.py:20
  267.7 7.2 %collective-permute-start.39 = (bf16[1,64,128]{2,1,0:T(8,128)(2,1)S(1)}, bf16[1,64,128]{2,1,0:T(8,128)(2,1)S(1)}, u32[]{:S(2)}, u32[]{:S(2)}) collective-permute-start(bf16[1,64,128]{2,1,0:T(8,128)(2,1)S(1)} %get-tuple-element.20), channel_id=1, source_target_pairs={{1,0},{2,1},{3,2},{4,3},{5,4},{6,5},{7,6},{8,7},{9,8},{10,9},{11,1... | collective-permute-start | bytes 49160 | tf_op jit(solution)/shard_map/ppermute | solution.py:22
  276.6 4.5 %collective-permute-start.40 = (bf16[1,64,128]{2,1,0:T(8,128)(2,1)S(1)}, bf16[1,64,128]{2,1,0:T(8,128)(2,1)S(1)}, u32[]{:S(2)}, u32[]{:S(2)}) collective-permute-start(bf16[1,64,128]{2,1,0:T(8,128)(2,1)S(1)} %get-tuple-element.17), channel_id=1, source_target_pairs={{0,1},{1,2},{2,3},{3,4},{4,5},{5,6},{6,7},{7,8},{8,9},{9,10},{10,1... | collective-permute-start | bytes 49160 | tf_op jit(solution)/shard_map/ppermute | solution.py:20
  278.6 7.2 %collective-permute-start.41 = (bf16[1,64,128]{2,1,0:T(8,128)(2,1)S(1)}, bf16[1,64,128]{2,1,0:T(8,128)(2,1)S(1)}, u32[]{:S(2)}, u32[]{:S(2)}) collective-permute-start(bf16[1,64,128]{2,1,0:T(8,128)(2,1)S(1)} %get-tuple-element.18), channel_id=1, source_target_pairs={{1,0},{2,1},{3,2},{4,3},{5,4},{6,5},{7,6},{8,7},{9,8},{10,9},{11,1... | collective-permute-start | bytes 49160 | tf_op jit(solution)/shard_map/ppermute | solution.py:22
  288.4 4.3 %collective-permute-start.42 = (bf16[1,128,128]{2,1,0:T(8,128)(2,1)S(1)}, bf16[1,128,128]{2,1,0:T(8,128)(2,1)S(1)}, u32[]{:S(2)}, u32[]{:S(2)}) collective-permute-start(bf16[1,128,128]{2,1,0:T(8,128)(2,1)S(1)} %get-tuple-element.7), channel_id=1, source_target_pairs={{0,1},{1,2},{2,3},{3,4},{4,5},{5,6},{6,7},{7,8},{8,9},{9,10},{10,1... | collective-permute-start | bytes 98312 | tf_op jit(solution)/shard_map/ppermute | solution.py:20
  290.3 7.3 %collective-permute-start.43 = (bf16[1,128,128]{2,1,0:T(8,128)(2,1)S(1)}, bf16[1,128,128]{2,1,0:T(8,128)(2,1)S(1)}, u32[]{:S(2)}, u32[]{:S(2)}) collective-permute-start(bf16[1,128,128]{2,1,0:T(8,128)(2,1)S(1)} %get-tuple-element.8), channel_id=1, source_target_pairs={{1,0},{2,1},{3,2},{4,3},{5,4},{6,5},{7,6},{8,7},{9,8},{10,9},{11,1... | collective-permute-start | bytes 98312 | tf_op jit(solution)/shard_map/ppermute | solution.py:22
  299.8 4.3 %collective-permute-start.44 = (bf16[1,128,128]{2,1,0:T(8,128)(2,1)S(1)}, bf16[1,128,128]{2,1,0:T(8,128)(2,1)S(1)}, u32[]{:S(2)}, u32[]{:S(2)}) collective-permute-start(bf16[1,128,128]{2,1,0:T(8,128)(2,1)S(1)} %get-tuple-element.5), channel_id=1, source_target_pairs={{0,1},{1,2},{2,3},{3,4},{4,5},{5,6},{6,7},{7,8},{8,9},{9,10},{10,1... | collective-permute-start | bytes 98312 | tf_op jit(solution)/shard_map/ppermute | solution.py:20
  301.8 7.3 %collective-permute-start.45 = (bf16[1,128,128]{2,1,0:T(8,128)(2,1)S(1)}, bf16[1,128,128]{2,1,0:T(8,128)(2,1)S(1)}, u32[]{:S(2)}, u32[]{:S(2)}) collective-permute-start(bf16[1,128,128]{2,1,0:T(8,128)(2,1)S(1)} %get-tuple-element.6), channel_id=1, source_target_pairs={{1,0},{2,1},{3,2},{4,3},{5,4},{6,5},{7,6},{8,7},{9,8},{10,9},{11,1... | collective-permute-start | bytes 98312 | tf_op jit(solution)/shard_map/ppermute | solution.py:22
where the time goes:
time: 313 us; the launch traced here: 312 us
  starting transfers between devices  128 us (41%)
  waiting for transfers between devices  105 us (34%)
  blocking collectives  35 us (11%)
  matrix products  31.9 us (10%)
  local copies, waits for them, and re-layouts  8.36 us (3%)
    ppermute x23, waiting for transfers between devices, with_halo(): lax.ppermute(head, axis, [((i + 1) % count, i) for i in range(ends)])  104 us
    ppermute x23, starting transfers between devices, with_halo(): lax.ppermute(tail, axis, [(i, (i + 1) % count) for i in range(ends)])  80.6 us
    ppermute x23, starting transfers between devices, with_halo(): lax.ppermute(head, axis, [((i + 1) % count, i) for i in range(ends)])  47.4 us
    all_gather x1, blocking collectives, shards(): reg_mean = lax.all_gather(mean_strip, 'ens', axis=2, tiled=True)  35 us
    dot_general x81, matrix products, conv_feat(): jnp.dot(window, weight[tap_y, tap_x], preferred_element_type=jnp.float32)  13 us
    dot_general x27, matrix products, conv_fields(): jnp.einsum('crw,co->rwo', window, weight[tap_y, tap_x], preferred_element...  7.14 us
    dot_general x48, matrix products, parity(): jnp.dot(window, weight[kernel_y, kernel_x], preferred_element_type=jnp.fl...  6.79 us
  transfers between devices with their start and end apart: 46, of which 23 were waited for; matrix products, arithmetic and copies ran while one was open for 1% of the time, Pallas kernels for 0%

commit v1 on v0

--- a/solution.py
+++ b/solution.py
@@ -147,7 +147,9 @@
     strip_start = lax.axis_index("ens") * strip_width
     strip_input = lax.dynamic_slice_in_dim(cond_padded, strip_start, strip_width + 2, 2)
     mean_strip = network_pass(strip_input, reg_weights, strip_pad, lower_each)
-    reg_mean = lax.all_gather(mean_strip, "ens", axis=2, tiled=True)
+    reg_mean = jnp.concatenate(
+        lax.all_to_all(jnp.stack([mean_strip] * lax.axis_size("ens")), "ens", 0, 0), axis=2
+    )
     mean_input = reg_mean.astype(jnp.bfloat16)
     residual_field = sigma_top * member_noise[0]
     for step_index in range(STEPS):

time: 313 us -> 294 us (0.939)
  blocking collectives: 35 us -> 0 us
  waiting for transfers between devices: 105 us -> 114 us
  starting transfers between devices: 128 us -> 133 us
    all_gather x1 -> x0, blocking collectives: 35 us -> none  [shards(): reg_mean = lax.all_gather(mean_strip, 'ens', axis=2, tiled=True)]
    all_to_all x0 -> x1, starting transfers between devices: none -> 10.2 us  [shards(): lax.all_to_all(jnp.stack([mean_strip] * lax.axis_size('ens')), 'ens', 0, 0)]
    all_to_all x0 -> x1, waiting for transfers between devices: none -> 8.88 us  [shards(): lax.all_to_all(jnp.stack([mean_strip] * lax.axis_size('ens')), 'ens', 0, 0)]
    ppermute x23, starting transfers between devices: 80.6 us -> 74.9 us  [with_halo(): lax.ppermute(tail, axis, [(i, (i + 1) % count) for i in range(ends)])]
  transfers between devices with their start and end apart: 46 -> 47, of which waited for: 23 -> 24; matrix products, arithmetic and copies ran while one was open for 1% -> 1% of each run, Pallas kernels for 0% -> 0%
where the time goes in v1:
time: 294 us; the launch traced here: 292 us
  starting transfers between devices  133 us (45%)
  waiting for transfers between devices  114 us (39%)
  matrix products  31.9 us (11%)
  local copies, waits for them, and re-layouts  9.97 us (3%)
    ppermute x23, waiting for transfers between devices, with_halo(): lax.ppermute(head, axis, [((i + 1) % count, i) for i in range(ends)])  104 us
    ppermute x23, starting transfers between devices, with_halo(): lax.ppermute(tail, axis, [(i, (i + 1) % count) for i in range(ends)])  74.9 us
    ppermute x23, starting transfers between devices, with_halo(): lax.ppermute(head, axis, [((i + 1) % count, i) for i in range(ends)])  47.5 us
    dot_general x81, matrix products, conv_feat(): jnp.dot(window, weight[tap_y, tap_x], preferred_element_type=jnp.float32)  13 us
    all_to_all x1, starting transfers between devices, shards(): lax.all_to_all(jnp.stack([mean_strip] * lax.axis_size('ens')), 'ens', 0, 0)  10.2 us
    all_to_all x1, waiting for transfers between devices, shards(): lax.all_to_all(jnp.stack([mean_strip] * lax.axis_size('ens')), 'ens', 0, 0)  8.88 us
    dot_general x27, matrix products, conv_fields(): jnp.einsum('crw,co->rwo', window, weight[tap_y, tap_x], preferred_element...  7.13 us
    dot_general x48, matrix products, parity(): jnp.dot(window, weight[kernel_y, kernel_x], preferred_element_type=jnp.fl...  6.79 us
  transfers between devices with their start and end apart: 47, of which 24 were waited for; matrix products, arithmetic and copies ran while one was open for 1% of the time, Pallas kernels for 0%

profile of v1, /device:TPU:27, one launch (start us, length us, event | category | flops | bytes accessed | tf_op | source)
XLA Modules:
  0.0 292.3 jit_solution(14985445322803164407)
XLA Ops:
  1.0 2.7 collective-permute-start.1
  3.8 5.1 %collective-permute-start = (bf16[12,1,128]{0,2,1:T(8,128)(2,1)S(1)}, bf16[12,1,128]{0,2,1:T(8,128)(2,1)S(1)}, u32[]{:S(2)}, u32[]{:S(2)}) collective-permute-start(bf16[12,1,128]{0,2,1:T(8,128)(2,1)S(1)} %copy.53), channel_id=1, source_target_pairs={{0,1},{1,2},{2,3},{3,4},{4,5},{5,6},{6,7},{7,8},{8,9},{9,10},{10,1... | collective-permute-start | bytes 9224 | tf_op jit(solution)/shard_map/ppermute | solution.py:20
  11.5 3.7 %collective-permute-start.2 = (bf16[8,1,128]{2,1,0:T(2,128)(2,1)S(1)}, bf16[8,1,128]{2,1,0:T(2,128)(2,1)S(1)}, u32[]{:S(2)}, u32[]{:S(2)}) collective-permute-start(bf16[8,1,128]{2,1,0:T(2,128)(2,1)S(1)} %get-tuple-element.45), channel_id=1, source_target_pairs={{0,32},{32,64},{64,96},{96,128},{128,160},{160,192},{192,224},{224... | collective-permute-start | bytes 6152 | tf_op jit(solution)/shard_map/ppermute | solution.py:20
  17.1 4.0 %collective-permute-done.3 = bf16[8,1,128]{2,1,0:T(2,128)(2,1)S(1)} collective-permute-done((bf16[8,1,128]{2,1,0:T(2,128)(2,1)S(1)}, bf16[8,1,128]{2,1,0:T(2,128)(2,1)S(1)}, u32[]{:S(2)}, u32[]{:S(2)}) %collective-permute-start.3) | collective-permute-done | bytes 2080 | tf_op jit(solution)/shard_map/ppermute | solution.py:22
  21.2 8.4 %collective-permute-start.4 = (bf16[1,10,128]{2,1,0:T(8,128)(2,1)S(1)}, bf16[1,10,128]{2,1,0:T(8,128)(2,1)S(1)}, u32[]{:S(2)}, u32[]{:S(2)}) collective-permute-start(bf16[1,10,128]{2,1,0:T(8,128)(2,1)S(1)} %get-tuple-element.29), channel_id=1, source_target_pairs={{0,1},{1,2},{2,3},{3,4},{4,5},{5,6},{6,7},{7,8},{8,9},{9,10},{10,1... | collective-permute-start | bytes 7688 | tf_op jit(solution)/shard_map/ppermute | solution.py:20
  29.6 1.9 collective-permute-start.5
  31.8 4.8 %collective-permute-done.5 = bf16[1,10,128]{2,1,0:T(8,128)(2,1)S(1)} collective-permute-done((bf16[1,10,128]{2,1,0:T(8,128)(2,1)S(1)}, bf16[1,10,128]{2,1,0:T(8,128)(2,1)S(1)}, u32[]{:S(2)}, u32[]{:S(2)}) %collective-permute-start.5) | collective-permute-done | bytes 2592 | tf_op jit(solution)/shard_map/ppermute | solution.py:22
  37.9 4.5 %collective-permute-start.6 = (bf16[4,1,128]{2,1,0:T(2,128)(2,1)S(1)}, bf16[4,1,128]{2,1,0:T(2,128)(2,1)S(1)}, u32[]{:S(2)}, u32[]{:S(2)}) collective-permute-start(bf16[4,1,128]{2,1,0:T(2,128)(2,1)S(1)} %get-tuple-element.57), channel_id=1, source_target_pairs={{0,32},{32,64},{64,96},{96,128},{128,160},{160,192},{192,224},{224... | collective-permute-start | bytes 3080 | tf_op jit(solution)/shard_map/ppermute | solution.py:20
  43.9 4.4 %collective-permute-done.7 = bf16[4,1,128]{2,1,0:T(2,128)(2,1)S(1)} collective-permute-done((bf16[4,1,128]{2,1,0:T(2,128)(2,1)S(1)}, bf16[4,1,128]{2,1,0:T(2,128)(2,1)S(1)}, u32[]{:S(2)}, u32[]{:S(2)}) %collective-permute-start.7) | collective-permute-done | bytes 1056 | tf_op jit(solution)/shard_map/ppermute | solution.py:22
  48.3 4.0 %collective-permute-start.8 = (bf16[1,6,128]{2,1,0:T(8,128)(2,1)S(1)}, bf16[1,6,128]{2,1,0:T(8,128)(2,1)S(1)}, u32[]{:S(2)}, u32[]{:S(2)}) collective-permute-start(bf16[1,6,128]{2,1,0:T(8,128)(2,1)S(1)} %get-tuple-element.53), channel_id=1, source_target_pairs={{0,1},{1,2},{2,3},{3,4},{4,5},{5,6},{6,7},{7,8},{8,9},{9,10},{10,1... | collective-permute-start | bytes 4616 | tf_op jit(solution)/shard_map/ppermute | solution.py:20
  52.3 1.9 collective-permute-start.9
  54.3 4.9 %collective-permute-done.9 = bf16[1,6,128]{2,1,0:T(8,128)(2,1)S(1)} collective-permute-done((bf16[1,6,128]{2,1,0:T(8,128)(2,1)S(1)}, bf16[1,6,128]{2,1,0:T(8,128)(2,1)S(1)}, u32[]{:S(2)}, u32[]{:S(2)}) %collective-permute-start.9) | collective-permute-done | bytes 1568 | tf_op jit(solution)/shard_map/ppermute | solution.py:22
  60.7 3.8 %collective-permute-start.10 = (bf16[4,1,128]{2,1,0:T(2,128)(2,1)S(1)}, bf16[4,1,128]{2,1,0:T(2,128)(2,1)S(1)}, u32[]{:S(2)}, u32[]{:S(2)}) collective-permute-start(bf16[4,1,128]{2,1,0:T(2,128)(2,1)S(1)} %get-tuple-element.55), channel_id=1, source_target_pairs={{0,32},{32,64},{64,96},{96,128},{128,160},{160,192},{192,224},{224... | collective-permute-start | bytes 3080 | tf_op jit(solution)/shard_map/ppermute | solution.py:20
  65.9 4.4 %collective-permute-done.11 = bf16[4,1,128]{2,1,0:T(2,128)(2,1)S(1)} collective-permute-done((bf16[4,1,128]{2,1,0:T(2,128)(2,1)S(1)}, bf16[4,1,128]{2,1,0:T(2,128)(2,1)S(1)}, u32[]{:S(2)}, u32[]{:S(2)}) %collective-permute-start.11) | collective-permute-done | bytes 1056 | tf_op jit(solution)/shard_map/ppermute | solution.py:22
  70.3 4.0 %collective-permute-start.12 = (bf16[1,6,128]{2,1,0:T(8,128)(2,1)S(1)}, bf16[1,6,128]{2,1,0:T(8,128)(2,1)S(1)}, u32[]{:S(2)}, u32[]{:S(2)}) collective-permute-start(bf16[1,6,128]{2,1,0:T(8,128)(2,1)S(1)} %get-tuple-element.49), channel_id=1, source_target_pairs={{0,1},{1,2},{2,3},{3,4},{4,5},{5,6},{6,7},{7,8},{8,9},{9,10},{10,1... | collective-permute-start | bytes 4616 | tf_op jit(solution)/shard_map/ppermute | solution.py:20
  74.3 1.9 collective-permute-start.13
  76.5 4.8 %collective-permute-done.13 = bf16[1,6,128]{2,1,0:T(8,128)(2,1)S(1)} collective-permute-done((bf16[1,6,128]{2,1,0:T(8,128)(2,1)S(1)}, bf16[1,6,128]{2,1,0:T(8,128)(2,1)S(1)}, u32[]{:S(2)}, u32[]{:S(2)}) %collective-permute-start.13) | collective-permute-done | bytes 1568 | tf_op jit(solution)/shard_map/ppermute | solution.py:22
  82.8 4.5 %collective-permute-start.14 = (bf16[8,1,128]{2,1,0:T(2,128)(2,1)S(1)}, bf16[8,1,128]{2,1,0:T(2,128)(2,1)S(1)}, u32[]{:S(2)}, u32[]{:S(2)}) collective-permute-start(bf16[8,1,128]{2,1,0:T(2,128)(2,1)S(1)} %get-tuple-element.43), channel_id=1, source_target_pairs={{0,32},{32,64},{64,96},{96,128},{128,160},{160,192},{192,224},{224... | collective-permute-start | bytes 6152 | tf_op jit(solution)/shard_map/ppermute | solution.py:20
  88.8 4.4 %collective-permute-done.15 = bf16[8,1,128]{2,1,0:T(2,128)(2,1)S(1)} collective-permute-done((bf16[8,1,128]{2,1,0:T(2,128)(2,1)S(1)}, bf16[8,1,128]{2,1,0:T(2,128)(2,1)S(1)}, u32[]{:S(2)}, u32[]{:S(2)}) %collective-permute-start.15) | collective-permute-done | bytes 2080 | tf_op jit(solution)/shard_map/ppermute | solution.py:22
  93.2 4.0 %collective-permute-start.16 = (bf16[1,10,128]{2,1,0:T(8,128)(2,1)S(1)}, bf16[1,10,128]{2,1,0:T(8,128)(2,1)S(1)}, u32[]{:S(2)}, u32[]{:S(2)}) collective-permute-start(bf16[1,10,128]{2,1,0:T(8,128)(2,1)S(1)} %get-tuple-element.37), channel_id=1, source_target_pairs={{0,1},{1,2},{2,3},{3,4},{4,5},{5,6},{6,7},{7,8},{8,9},{9,10},{10,1... | collective-permute-start | bytes 7688 | tf_op jit(solution)/shard_map/ppermute | solution.py:20
  97.2 1.9 collective-permute-start.17
  99.2 5.0 %collective-permute-done.17 = bf16[1,10,128]{2,1,0:T(8,128)(2,1)S(1)} collective-permute-done((bf16[1,10,128]{2,1,0:T(8,128)(2,1)S(1)}, bf16[1,10,128]{2,1,0:T(8,128)(2,1)S(1)}, u32[]{:S(2)}, u32[]{:S(2)}) %collective-permute-start.17) | collective-permute-done | bytes 2592 | tf_op jit(solution)/shard_map/ppermute | solution.py:22
  105.2 3.8 %collective-permute-start.18 = (bf16[8,1,128]{2,1,0:T(2,128)(2,1)S(1)}, bf16[8,1,128]{2,1,0:T(2,128)(2,1)S(1)}, u32[]{:S(2)}, u32[]{:S(2)}) collective-permute-start(bf16[8,1,128]{2,1,0:T(2,128)(2,1)S(1)} %get-tuple-element.41), channel_id=1, source_target_pairs={{0,32},{32,64},{64,96},{96,128},{128,160},{160,192},{192,224},{224... | collective-permute-start | bytes 6152 | tf_op jit(solution)/shard_map/ppermute | solution.py:20
  110.5 4.4 %collective-permute-done.19 = bf16[8,1,128]{2,1,0:T(2,128)(2,1)S(1)} collective-permute-done((bf16[8,1,128]{2,1,0:T(2,128)(2,1)S(1)}, bf16[8,1,128]{2,1,0:T(2,128)(2,1)S(1)}, u32[]{:S(2)}, u32[]{:S(2)}) %collective-permute-start.19) | collective-permute-done | bytes 2080 | tf_op jit(solution)/shard_map/ppermute | solution.py:22
  114.9 4.0 %collective-permute-start.20 = (bf16[1,10,128]{2,1,0:T(8,128)(2,1)S(1)}, bf16[1,10,128]{2,1,0:T(8,128)(2,1)S(1)}, u32[]{:S(2)}, u32[]{:S(2)}) collective-permute-start(bf16[1,10,128]{2,1,0:T(8,128)(2,1)S(1)} %get-tuple-element.33), channel_id=1, source_target_pairs={{0,1},{1,2},{2,3},{3,4},{4,5},{5,6},{6,7},{7,8},{8,9},{9,10},{10,1... | collective-permute-start | bytes 7688 | tf_op jit(solution)/shard_map/ppermute | solution.py:20
  118.9 1.9 collective-permute-start.21
  121.0 4.9 %collective-permute-done.21 = bf16[1,10,128]{2,1,0:T(8,128)(2,1)S(1)} collective-permute-done((bf16[1,10,128]{2,1,0:T(8,128)(2,1)S(1)}, bf16[1,10,128]{2,1,0:T(8,128)(2,1)S(1)}, u32[]{:S(2)}, u32[]{:S(2)}) %collective-permute-start.21) | collective-permute-done | bytes 2592 | tf_op jit(solution)/shard_map/ppermute | solution.py:22
  128.1 10.2 %all-to-all-start = ((f32[16,1,256]{2,1,0:T(1,128)}), f32[16,1,256]{2,1,0:T(1,128)S(1)}, u32[]{:S(2)}, u32[]{:S(2)}) async-start(f32[16,1,256]{2,1,0:T(1,128)} %reshape.145), calls=%async_computation | async-start | bytes 32768 | tf_op jit(solution)/shard_map/all_to_all | solution.py:151
  138.3 8.9 %all-to-all-done = f32[16,1,256]{2,1,0:T(1,128)S(1)} async-done(((f32[16,1,256]{2,1,0:T(1,128)}), f32[16,1,256]{2,1,0:T(1,128)S(1)}, u32[]{:S(2)}, u32[]{:S(2)}) %all-to-all-start) | async-done | bytes 16416 | tf_op jit(solution)/shard_map/all_to_all | solution.py:151
  149.0 4.0 %collective-permute-start.22 = (bf16[20,1,128]{2,0,1:T(8,128)(2,1)S(1)}, bf16[20,1,128]{2,0,1:T(8,128)(2,1)S(1)}, u32[]{:S(2)}, u32[]{:S(2)}) collective-permute-start(bf16[20,1,128]{2,0,1:T(8,128)(2,1)S(1)} %get-tuple-element.27), channel_id=1, source_target_pairs={{0,1},{1,2},{2,3},{3,4},{4,5},{5,6},{6,7},{7,8},{8,9},{9,10},{10,1... | collective-permute-start | bytes 15368 | tf_op jit(solution)/shard_map/ppermute | solution.py:20
  153.0 2.1 collective-permute-start.23
  155.0 5.1 %collective-permute-done.23 = bf16[20,1,128]{2,0,1:T(8,128)(2,1)S(1)} collective-permute-done((bf16[20,1,128]{2,0,1:T(8,128)(2,1)S(1)}, bf16[20,1,128]{2,0,1:T(8,128)(2,1)S(1)}, u32[]{:S(2)}, u32[]{:S(2)}) %collective-permute-start.23) | collective-permute-done | bytes 5152 | tf_op jit(solution)/shard_map/ppermute | solution.py:22
  163.3 2.0 collective-permute-start.24
  165.2 2.4 collective-permute-start.25
  167.6 4.9 %collective-permute-done.25 = bf16[1,128,128]{2,1,0:T(8,128)(2,1)S(1)} collective-permute-done((bf16[1,128,128]{2,1,0:T(8,128)(2,1)S(1)}, bf16[1,128,128]{2,1,0:T(8,128)(2,1)S(1)}, u32[]{:S(2)}, u32[]{:S(2)}) %collective-permute-start.25) | collective-permute-done | bytes 32800 | tf_op jit(solution)/shard_map/ppermute | solution.py:22
  175.9 1.9 collective-permute-start.26
  177.9 2.4 collective-permute-start.27
  180.3 4.7 %collective-permute-done.27 = bf16[1,64,128]{2,1,0:T(8,128)(2,1)S(1)} collective-permute-done((bf16[1,64,128]{2,1,0:T(8,128)(2,1)S(1)}, bf16[1,64,128]{2,1,0:T(8,128)(2,1)S(1)}, u32[]{:S(2)}, u32[]{:S(2)}) %collective-permute-start.27) | collective-permute-done | bytes 16416 | tf_op jit(solution)/shard_map/ppermute | solution.py:22
  187.6 1.9 collective-permute-start.28
  189.6 2.4 collective-permute-start.29
  192.1 4.6 %collective-permute-done.29 = bf16[1,64,128]{2,1,0:T(8,128)(2,1)S(1)} collective-permute-done((bf16[1,64,128]{2,1,0:T(8,128)(2,1)S(1)}, bf16[1,64,128]{2,1,0:T(8,128)(2,1)S(1)}, u32[]{:S(2)}, u32[]{:S(2)}) %collective-permute-start.29) | collective-permute-done | bytes 16416 | tf_op jit(solution)/shard_map/ppermute | solution.py:22
  199.4 1.9 collective-permute-start.30
  201.3 2.5 collective-permute-start.31
  203.9 4.9 %collective-permute-done.31 = bf16[1,128,128]{2,1,0:T(8,128)(2,1)S(1)} collective-permute-done((bf16[1,128,128]{2,1,0:T(8,128)(2,1)S(1)}, bf16[1,128,128]{2,1,0:T(8,128)(2,1)S(1)}, u32[]{:S(2)}, u32[]{:S(2)}) %collective-permute-start.31) | collective-permute-done | bytes 32800 | tf_op jit(solution)/shard_map/ppermute | solution.py:22
  211.0 1.9 collective-permute-start.32
  212.9 2.4 collective-permute-start.33
  215.4 4.9 %collective-permute-done.33 = bf16[1,128,128]{2,1,0:T(8,128)(2,1)S(1)} collective-permute-done((bf16[1,128,128]{2,1,0:T(8,128)(2,1)S(1)}, bf16[1,128,128]{2,1,0:T(8,128)(2,1)S(1)}, u32[]{:S(2)}, u32[]{:S(2)}) %collective-permute-start.33) | collective-permute-done | bytes 32800 | tf_op jit(solution)/shard_map/ppermute | solution.py:22
  222.1 1.9 collective-permute-start.34
  224.1 2.6 collective-permute-start.35
  226.7 4.5 %collective-permute-done.35 = bf16[20,1,128]{2,0,1:T(8,128)(2,1)S(1)} collective-permute-done((bf16[20,1,128]{2,0,1:T(8,128)(2,1)S(1)}, bf16[20,1,128]{2,0,1:T(8,128)(2,1)S(1)}, u32[]{:S(2)}, u32[]{:S(2)}) %collective-permute-start.35) | collective-permute-done | bytes 5152 | tf_op jit(solution)/shard_map/ppermute | solution.py:22
  234.2 1.9 collective-permute-start.36
  236.2 2.4 collective-permute-start.37
  238.6 4.9 %collective-permute-done.37 = bf16[1,128,128]{2,1,0:T(8,128)(2,1)S(1)} collective-permute-done((bf16[1,128,128]{2,1,0:T(8,128)(2,1)S(1)}, bf16[1,128,128]{2,1,0:T(8,128)(2,1)S(1)}, u32[]{:S(2)}, u32[]{:S(2)}) %collective-permute-start.37) | collective-permute-done | bytes 32800 | tf_op jit(solution)/shard_map/ppermute | solution.py:22
  248.5 2.4 collective-permute-start.39
  251.0 4.7 %collective-permute-done.39 = bf16[1,64,128]{2,1,0:T(8,128)(2,1)S(1)} collective-permute-done((bf16[1,64,128]{2,1,0:T(8,128)(2,1)S(1)}, bf16[1,64,128]{2,1,0:T(8,128)(2,1)S(1)}, u32[]{:S(2)}, u32[]{:S(2)}) %collective-permute-start.39) | collective-permute-done | bytes 16416 | tf_op jit(solution)/shard_map/ppermute | solution.py:22
  257.5 1.9 collective-permute-start.40
  259.4 2.4 collective-permute-start.41
  262.0 4.6 %collective-permute-done.41 = bf16[1,64,128]{2,1,0:T(8,128)(2,1)S(1)} collective-permute-done((bf16[1,64,128]{2,1,0:T(8,128)(2,1)S(1)}, bf16[1,64,128]{2,1,0:T(8,128)(2,1)S(1)}, u32[]{:S(2)}, u32[]{:S(2)}) %collective-permute-start.41) | collective-permute-done | bytes 16416 | tf_op jit(solution)/shard_map/ppermute | solution.py:22
  269.2 1.9 collective-permute-start.42
  271.1 2.4 collective-permute-start.43
  273.5 4.9 %collective-permute-done.43 = bf16[1,128,128]{2,1,0:T(8,128)(2,1)S(1)} collective-permute-done((bf16[1,128,128]{2,1,0:T(8,128)(2,1)S(1)}, bf16[1,128,128]{2,1,0:T(8,128)(2,1)S(1)}, u32[]{:S(2)}, u32[]{:S(2)}) %collective-permute-start.43) | collective-permute-done | bytes 32800 | tf_op jit(solution)/shard_map/ppermute | solution.py:22
  280.7 1.9 collective-permute-start.44
  282.6 2.4 collective-permute-start.45
  285.0 4.9 %collective-permute-done.45 = bf16[1,128,128]{2,1,0:T(8,128)(2,1)S(1)} collective-permute-done((bf16[1,128,128]{2,1,0:T(8,128)(2,1)S(1)}, bf16[1,128,128]{2,1,0:T(8,128)(2,1)S(1)}, u32[]{:S(2)}, u32[]{:S(2)}) %collective-permute-start.45) | collective-permute-done | bytes 32800 | tf_op jit(solution)/shard_map/ppermute | solution.py:22
  (341 shorter events, 53.3 us)
Async XLA Ops:
  1.0 8.0 %copy-start.9 = (bf16[12,8,128]{2,1,0:T(8,128)(2,1)S(1)}, bf16[12,8,128]{2,1,0:T(8,128)(2,1)}, u32[]{:S(2)}) copy-start(bf16[12,8,128]{2,1,0:T(8,128)(2,1)} %param.14) | copy-start | bytes 73732
  1.0 8.2 %collective-permute-start.1 = (bf16[12,1,128]{0,2,1:T(8,128)(2,1)S(1)}, bf16[12,1,128]{0,2,1:T(8,128)(2,1)S(1)}, u32[]{:S(2)}, u32[]{:S(2)}) collective-permute-start(bf16[12,1,128]{0,2,1:T(8,128)(2,1)S(1)} %copy.54), channel_id=1, source_target_pairs={{1,0},{2,1},{3,2},{4,3},{5,4},{6,5},{7,6},{8,7},{9,8},{10,9},{11,1... | collective-permute-start | bytes 9224 | tf_op jit(solution)/shard_map/ppermute | solution.py:22
  3.8 6.1 %collective-permute-start = (bf16[12,1,128]{0,2,1:T(8,128)(2,1)S(1)}, bf16[12,1,128]{0,2,1:T(8,128)(2,1)S(1)}, u32[]{:S(2)}, u32[]{:S(2)}) collective-permute-start(bf16[12,1,128]{0,2,1:T(8,128)(2,1)S(1)} %copy.53), channel_id=1, source_target_pairs={{0,1},{1,2},{2,3},{3,4},{4,5},{5,6},{6,7},{7,8},{8,9},{9,10},{10,1... | collective-permute-start | bytes 9224 | tf_op jit(solution)/shard_map/ppermute | solution.py:20
  9.1 0.8 copy-start.10
  10.5 6.0 %copy-start.6 = (bf16[3,3,128,128]{3,2,1,0:T(8,128)(2,1)S(1)}, bf16[3,3,128,128]{3,2,1,0:T(8,128)(2,1)}, u32[]{:S(2)}) copy-start(bf16[3,3,128,128]{3,2,1,0:T(8,128)(2,1)} %param.17) | copy-start | bytes 884740
  11.5 5.6 %collective-permute-start.2 = (bf16[8,1,128]{2,1,0:T(2,128)(2,1)S(1)}, bf16[8,1,128]{2,1,0:T(2,128)(2,1)S(1)}, u32[]{:S(2)}, u32[]{:S(2)}) collective-permute-start(bf16[8,1,128]{2,1,0:T(2,128)(2,1)S(1)} %get-tuple-element.45), channel_id=1, source_target_pairs={{0,32},{32,64},{64,96},{96,128},{128,160},{160,192},{192,224},{224... | collective-permute-start | bytes 6152 | tf_op jit(solution)/shard_map/ppermute | solution.py:20
  15.2 5.9 %collective-permute-start.3 = (bf16[8,1,128]{2,1,0:T(2,128)(2,1)S(1)}, bf16[8,1,128]{2,1,0:T(2,128)(2,1)S(1)}, u32[]{:S(2)}, u32[]{:S(2)}) collective-permute-start(bf16[8,1,128]{2,1,0:T(2,128)(2,1)S(1)} %get-tuple-element.46), channel_id=1, source_target_pairs={{32,0},{64,32},{96,64},{128,96},{160,128},{192,160},{224,192},{256... | collective-permute-start | bytes 6152 | tf_op jit(solution)/shard_map/ppermute | solution.py:22
  21.1 22.6 %copy-start.5 = (bf16[3,3,128,128]{3,2,1,0:T(8,128)(2,1)S(1)}, bf16[3,3,128,128]{3,2,1,0:T(8,128)(2,1)}, u32[]{:S(2)}) copy-start(bf16[3,3,128,128]{3,2,1,0:T(8,128)(2,1)} %param.18) | copy-start | bytes 884740
  21.2 10.6 %collective-permute-start.4 = (bf16[1,10,128]{2,1,0:T(8,128)(2,1)S(1)}, bf16[1,10,128]{2,1,0:T(8,128)(2,1)S(1)}, u32[]{:S(2)}, u32[]{:S(2)}) collective-permute-start(bf16[1,10,128]{2,1,0:T(8,128)(2,1)S(1)} %get-tuple-element.29), channel_id=1, source_target_pairs={{0,1},{1,2},{2,3},{3,4},{4,5},{5,6},{6,7},{7,8},{8,9},{9,10},{10,1... | collective-permute-start | bytes 7688 | tf_op jit(solution)/shard_map/ppermute | solution.py:20
  29.6 7.0 %collective-permute-start.5 = (bf16[1,10,128]{2,1,0:T(8,128)(2,1)S(1)}, bf16[1,10,128]{2,1,0:T(8,128)(2,1)S(1)}, u32[]{:S(2)}, u32[]{:S(2)}) collective-permute-start(bf16[1,10,128]{2,1,0:T(8,128)(2,1)S(1)} %get-tuple-element.30), channel_id=1, source_target_pairs={{1,0},{2,1},{3,2},{4,3},{5,4},{6,5},{7,6},{8,7},{9,8},{10,9},{11,1... | collective-permute-start | bytes 7688 | tf_op jit(solution)/shard_map/ppermute | solution.py:22
  36.7 23.6 %copy-start.4 = (bf16[4,4,128,128]{3,2,1,0:T(8,128)(2,1)S(1)}, bf16[4,4,128,128]{3,2,1,0:T(8,128)(2,1)}, u32[]{:S(2)}) copy-start(bf16[4,4,128,128]{3,2,1,0:T(8,128)(2,1)} %param.19) | copy-start | bytes 1572868
  37.9 6.0 %collective-permute-start.6 = (bf16[4,1,128]{2,1,0:T(2,128)(2,1)S(1)}, bf16[4,1,128]{2,1,0:T(2,128)(2,1)S(1)}, u32[]{:S(2)}, u32[]{:S(2)}) collective-permute-start(bf16[4,1,128]{2,1,0:T(2,128)(2,1)S(1)} %get-tuple-element.57), channel_id=1, source_target_pairs={{0,32},{32,64},{64,96},{96,128},{128,160},{160,192},{192,224},{224... | collective-permute-start | bytes 3080 | tf_op jit(solution)/shard_map/ppermute | solution.py:20
  42.4 5.8 %collective-permute-start.7 = (bf16[4,1,128]{2,1,0:T(2,128)(2,1)S(1)}, bf16[4,1,128]{2,1,0:T(2,128)(2,1)S(1)}, u32[]{:S(2)}, u32[]{:S(2)}) collective-permute-start(bf16[4,1,128]{2,1,0:T(2,128)(2,1)S(1)} %get-tuple-element.58), channel_id=1, source_target_pairs={{32,0},{64,32},{96,64},{128,96},{160,128},{192,160},{224,192},{256... | collective-permute-start | bytes 3080 | tf_op jit(solution)/shard_map/ppermute | solution.py:22
  48.3 6.1 %collective-permute-start.8 = (bf16[1,6,128]{2,1,0:T(8,128)(2,1)S(1)}, bf16[1,6,128]{2,1,0:T(8,128)(2,1)S(1)}, u32[]{:S(2)}, u32[]{:S(2)}) collective-permute-start(bf16[1,6,128]{2,1,0:T(8,128)(2,1)S(1)} %get-tuple-element.53), channel_id=1, source_target_pairs={{0,1},{1,2},{2,3},{3,4},{4,5},{5,6},{6,7},{7,8},{8,9},{9,10},{10,1... | collective-permute-start | bytes 4616 | tf_op jit(solution)/shard_map/ppermute | solution.py:20
  52.3 7.0 %collective-permute-start.9 = (bf16[1,6,128]{2,1,0:T(8,128)(2,1)S(1)}, bf16[1,6,128]{2,1,0:T(8,128)(2,1)S(1)}, u32[]{:S(2)}, u32[]{:S(2)}) collective-permute-start(bf16[1,6,128]{2,1,0:T(8,128)(2,1)S(1)} %get-tuple-element.54), channel_id=1, source_target_pairs={{1,0},{2,1},{3,2},{4,3},{5,4},{6,5},{7,6},{8,7},{9,8},{10,9},{11,1... | collective-permute-start | bytes 4616 | tf_op jit(solution)/shard_map/ppermute | solution.py:22
  60.7 5.2 %collective-permute-start.10 = (bf16[4,1,128]{2,1,0:T(2,128)(2,1)S(1)}, bf16[4,1,128]{2,1,0:T(2,128)(2,1)S(1)}, u32[]{:S(2)}, u32[]{:S(2)}) collective-permute-start(bf16[4,1,128]{2,1,0:T(2,128)(2,1)S(1)} %get-tuple-element.55), channel_id=1, source_target_pairs={{0,32},{32,64},{64,96},{96,128},{128,160},{160,192},{192,224},{224... | collective-permute-start | bytes 3080 | tf_op jit(solution)/shard_map/ppermute | solution.py:20
  64.4 5.8 %collective-permute-start.11 = (bf16[4,1,128]{2,1,0:T(2,128)(2,1)S(1)}, bf16[4,1,128]{2,1,0:T(2,128)(2,1)S(1)}, u32[]{:S(2)}, u32[]{:S(2)}) collective-permute-start(bf16[4,1,128]{2,1,0:T(2,128)(2,1)S(1)} %get-tuple-element.56), channel_id=1, source_target_pairs={{32,0},{64,32},{96,64},{128,96},{160,128},{192,160},{224,192},{256... | collective-permute-start | bytes 3080 | tf_op jit(solution)/shard_map/ppermute | solution.py:22
  70.3 6.2 %collective-permute-start.12 = (bf16[1,6,128]{2,1,0:T(8,128)(2,1)S(1)}, bf16[1,6,128]{2,1,0:T(8,128)(2,1)S(1)}, u32[]{:S(2)}, u32[]{:S(2)}) collective-permute-start(bf16[1,6,128]{2,1,0:T(8,128)(2,1)S(1)} %get-tuple-element.49), channel_id=1, source_target_pairs={{0,1},{1,2},{2,3},{3,4},{4,5},{5,6},{6,7},{7,8},{8,9},{9,10},{10,1... | collective-permute-start | bytes 4616 | tf_op jit(solution)/shard_map/ppermute | solution.py:20
  74.3 7.0 %collective-permute-start.13 = (bf16[1,6,128]{2,1,0:T(8,128)(2,1)S(1)}, bf16[1,6,128]{2,1,0:T(8,128)(2,1)S(1)}, u32[]{:S(2)}, u32[]{:S(2)}) collective-permute-start(bf16[1,6,128]{2,1,0:T(8,128)(2,1)S(1)} %get-tuple-element.50), channel_id=1, source_target_pairs={{1,0},{2,1},{3,2},{4,3},{5,4},{6,5},{7,6},{8,7},{9,8},{10,9},{11,1... | collective-permute-start | bytes 4616 | tf_op jit(solution)/shard_map/ppermute | solution.py:22
  82.0 6.6 %copy-start.7 = (bf16[3,3,128,128]{3,2,1,0:T(8,128)(2,1)S(1)}, bf16[3,3,128,128]{3,2,1,0:T(8,128)(2,1)}, u32[]{:S(2)}) copy-start(bf16[3,3,128,128]{3,2,1,0:T(8,128)(2,1)} %param.20) | copy-start | bytes 884740
  82.8 6.0 %collective-permute-start.14 = (bf16[8,1,128]{2,1,0:T(2,128)(2,1)S(1)}, bf16[8,1,128]{2,1,0:T(2,128)(2,1)S(1)}, u32[]{:S(2)}, u32[]{:S(2)}) collective-permute-start(bf16[8,1,128]{2,1,0:T(2,128)(2,1)S(1)} %get-tuple-element.43), channel_id=1, source_target_pairs={{0,32},{32,64},{64,96},{96,128},{128,160},{160,192},{192,224},{224... | collective-permute-start | bytes 6152 | tf_op jit(solution)/shard_map/ppermute | solution.py:20
  87.3 5.9 %collective-permute-start.15 = (bf16[8,1,128]{2,1,0:T(2,128)(2,1)S(1)}, bf16[8,1,128]{2,1,0:T(2,128)(2,1)S(1)}, u32[]{:S(2)}, u32[]{:S(2)}) collective-permute-start(bf16[8,1,128]{2,1,0:T(2,128)(2,1)S(1)} %get-tuple-element.44), channel_id=1, source_target_pairs={{32,0},{64,32},{96,64},{128,96},{160,128},{192,160},{224,192},{256... | collective-permute-start | bytes 6152 | tf_op jit(solution)/shard_map/ppermute | solution.py:22
  93.2 6.1 %collective-permute-start.16 = (bf16[1,10,128]{2,1,0:T(8,128)(2,1)S(1)}, bf16[1,10,128]{2,1,0:T(8,128)(2,1)S(1)}, u32[]{:S(2)}, u32[]{:S(2)}) collective-permute-start(bf16[1,10,128]{2,1,0:T(8,128)(2,1)S(1)} %get-tuple-element.37), channel_id=1, source_target_pairs={{0,1},{1,2},{2,3},{3,4},{4,5},{5,6},{6,7},{7,8},{8,9},{9,10},{10,1... | collective-permute-start | bytes 7688 | tf_op jit(solution)/shard_map/ppermute | solution.py:20
  97.2 7.0 %collective-permute-start.17 = (bf16[1,10,128]{2,1,0:T(8,128)(2,1)S(1)}, bf16[1,10,128]{2,1,0:T(8,128)(2,1)S(1)}, u32[]{:S(2)}, u32[]{:S(2)}) collective-permute-start(bf16[1,10,128]{2,1,0:T(8,128)(2,1)S(1)} %get-tuple-element.38), channel_id=1, source_target_pairs={{1,0},{2,1},{3,2},{4,3},{5,4},{6,5},{7,6},{8,7},{9,8},{10,9},{11,1... | collective-permute-start | bytes 7688 | tf_op jit(solution)/shard_map/ppermute | solution.py:22
  105.2 5.1 %copy-start.12 = (bf16[3,3,4,128]{3,2,1,0:T(4,128)(2,1)S(1)}, bf16[3,3,4,128]{3,2,1,0:T(4,128)(2,1)}, u32[]{:S(2)}) copy-start(bf16[3,3,4,128]{3,2,1,0:T(4,128)(2,1)} %param.21) | copy-start | bytes 27652
  105.2 5.2 %collective-permute-start.18 = (bf16[8,1,128]{2,1,0:T(2,128)(2,1)S(1)}, bf16[8,1,128]{2,1,0:T(2,128)(2,1)S(1)}, u32[]{:S(2)}, u32[]{:S(2)}) collective-permute-start(bf16[8,1,128]{2,1,0:T(2,128)(2,1)S(1)} %get-tuple-element.41), channel_id=1, source_target_pairs={{0,32},{32,64},{64,96},{96,128},{128,160},{160,192},{192,224},{224... | collective-permute-start | bytes 6152 | tf_op jit(solution)/shard_map/ppermute | solution.py:20
  109.0 5.9 %collective-permute-start.19 = (bf16[8,1,128]{2,1,0:T(2,128)(2,1)S(1)}, bf16[8,1,128]{2,1,0:T(2,128)(2,1)S(1)}, u32[]{:S(2)}, u32[]{:S(2)}) collective-permute-start(bf16[8,1,128]{2,1,0:T(2,128)(2,1)S(1)} %get-tuple-element.42), channel_id=1, source_target_pairs={{32,0},{64,32},{96,64},{128,96},{160,128},{192,160},{224,192},{256... | collective-permute-start | bytes 6152 | tf_op jit(solution)/shard_map/ppermute | solution.py:22
  114.9 6.1 %collective-permute-start.20 = (bf16[1,10,128]{2,1,0:T(8,128)(2,1)S(1)}, bf16[1,10,128]{2,1,0:T(8,128)(2,1)S(1)}, u32[]{:S(2)}, u32[]{:S(2)}) collective-permute-start(bf16[1,10,128]{2,1,0:T(8,128)(2,1)S(1)} %get-tuple-element.33), channel_id=1, source_target_pairs={{0,1},{1,2},{2,3},{3,4},{4,5},{5,6},{6,7},{7,8},{8,9},{9,10},{10,1... | collective-permute-start | bytes 7688 | tf_op jit(solution)/shard_map/ppermute | solution.py:20
  118.9 7.0 %collective-permute-start.21 = (bf16[1,10,128]{2,1,0:T(8,128)(2,1)S(1)}, bf16[1,10,128]{2,1,0:T(8,128)(2,1)S(1)}, u32[]{:S(2)}, u32[]{:S(2)}) collective-permute-start(bf16[1,10,128]{2,1,0:T(8,128)(2,1)S(1)} %get-tuple-element.34), channel_id=1, source_target_pairs={{1,0},{2,1},{3,2},{4,3},{5,4},{6,5},{7,6},{8,7},{9,8},{10,9},{11,1... | collective-permute-start | bytes 7688 | tf_op jit(solution)/shard_map/ppermute | solution.py:22
  128.1 10.2 %copy-start.11 = (f32[1,4,8,128]{3,2,1,0:T(8,128)S(1)}, f32[1,4,8,128]{3,2,1,0:T(8,128)}, u32[]{:S(2)}) copy-start(f32[1,4,8,128]{3,2,1,0:T(8,128)} %param.15) | copy-start | bytes 49156
  128.1 19.1 %all-to-all-start = ((f32[16,1,256]{2,1,0:T(1,128)}), f32[16,1,256]{2,1,0:T(1,128)S(1)}, u32[]{:S(2)}, u32[]{:S(2)}) async-start(f32[16,1,256]{2,1,0:T(1,128)} %reshape.145), calls=%async_computation | async-start | bytes 32768 | tf_op jit(solution)/shard_map/all_to_all | solution.py:151
  149.0 6.1 %collective-permute-start.22 = (bf16[20,1,128]{2,0,1:T(8,128)(2,1)S(1)}, bf16[20,1,128]{2,0,1:T(8,128)(2,1)S(1)}, u32[]{:S(2)}, u32[]{:S(2)}) collective-permute-start(bf16[20,1,128]{2,0,1:T(8,128)(2,1)S(1)} %get-tuple-element.27), channel_id=1, source_target_pairs={{0,1},{1,2},{2,3},{3,4},{4,5},{5,6},{6,7},{7,8},{8,9},{9,10},{10,1... | collective-permute-start | bytes 15368 | tf_op jit(solution)/shard_map/ppermute | solution.py:20
  152.9 7.2 %copy-start.8 = (bf16[3,3,20,128]{3,2,1,0:T(8,128)(2,1)S(1)}, bf16[3,3,20,128]{3,2,1,0:T(8,128)(2,1)}, u32[]{:S(2)}) copy-start(bf16[3,3,20,128]{3,2,1,0:T(8,128)(2,1)} %param.22) | copy-start | bytes 138244
  153.0 7.2 %collective-permute-start.23 = (bf16[20,1,128]{2,0,1:T(8,128)(2,1)S(1)}, bf16[20,1,128]{2,0,1:T(8,128)(2,1)S(1)}, u32[]{:S(2)}, u32[]{:S(2)}) collective-permute-start(bf16[20,1,128]{2,0,1:T(8,128)(2,1)S(1)} %get-tuple-element.28), channel_id=1, source_target_pairs={{1,0},{2,1},{3,2},{4,3},{5,4},{6,5},{7,6},{8,7},{9,8},{10,9},{11,1... | collective-permute-start | bytes 15368 | tf_op jit(solution)/shard_map/ppermute | solution.py:22
  163.3 4.3 %collective-permute-start.24 = (bf16[1,128,128]{2,1,0:T(8,128)(2,1)S(1)}, bf16[1,128,128]{2,1,0:T(8,128)(2,1)S(1)}, u32[]{:S(2)}, u32[]{:S(2)}) collective-permute-start(bf16[1,128,128]{2,1,0:T(8,128)(2,1)S(1)} %get-tuple-element.15), channel_id=1, source_target_pairs={{0,1},{1,2},{2,3},{3,4},{4,5},{5,6},{6,7},{7,8},{8,9},{9,10},{10,1... | collective-permute-start | bytes 98312 | tf_op jit(solution)/shard_map/ppermute | solution.py:20
  165.2 7.3 %collective-permute-start.25 = (bf16[1,128,128]{2,1,0:T(8,128)(2,1)S(1)}, bf16[1,128,128]{2,1,0:T(8,128)(2,1)S(1)}, u32[]{:S(2)}, u32[]{:S(2)}) collective-permute-start(bf16[1,128,128]{2,1,0:T(8,128)(2,1)S(1)} %get-tuple-element.16), channel_id=1, source_target_pairs={{1,0},{2,1},{3,2},{4,3},{5,4},{6,5},{7,6},{8,7},{9,8},{10,9},{11,1... | collective-permute-start | bytes 98312 | tf_op jit(solution)/shard_map/ppermute | solution.py:22
  173.6 1.0 copy-start.2
  175.7 9.3 %copy-start.1 = (bf16[3,3,128,128]{3,2,1,0:T(8,128)(2,1)S(1)}, bf16[3,3,128,128]{3,2,1,0:T(8,128)(2,1)}, u32[]{:S(2)}) copy-start(bf16[3,3,128,128]{3,2,1,0:T(8,128)(2,1)} %param.24) | copy-start | bytes 884740
  175.9 4.3 %collective-permute-start.26 = (bf16[1,64,128]{2,1,0:T(8,128)(2,1)S(1)}, bf16[1,64,128]{2,1,0:T(8,128)(2,1)S(1)}, u32[]{:S(2)}, u32[]{:S(2)}) collective-permute-start(bf16[1,64,128]{2,1,0:T(8,128)(2,1)S(1)} %get-tuple-element.23), channel_id=1, source_target_pairs={{0,1},{1,2},{2,3},{3,4},{4,5},{5,6},{6,7},{7,8},{8,9},{9,10},{10,1... | collective-permute-start | bytes 49160 | tf_op jit(solution)/shard_map/ppermute | solution.py:20
  177.9 7.2 %collective-permute-start.27 = (bf16[1,64,128]{2,1,0:T(8,128)(2,1)S(1)}, bf16[1,64,128]{2,1,0:T(8,128)(2,1)S(1)}, u32[]{:S(2)}, u32[]{:S(2)}) collective-permute-start(bf16[1,64,128]{2,1,0:T(8,128)(2,1)S(1)} %get-tuple-element.24), channel_id=1, source_target_pairs={{1,0},{2,1},{3,2},{4,3},{5,4},{6,5},{7,6},{8,7},{9,8},{10,9},{11,1... | collective-permute-start | bytes 49160 | tf_op jit(solution)/shard_map/ppermute | solution.py:22
  186.3 1.0 copy-start
  187.6 4.5 %collective-permute-start.28 = (bf16[1,64,128]{2,1,0:T(8,128)(2,1)S(1)}, bf16[1,64,128]{2,1,0:T(8,128)(2,1)S(1)}, u32[]{:S(2)}, u32[]{:S(2)}) collective-permute-start(bf16[1,64,128]{2,1,0:T(8,128)(2,1)S(1)} %get-tuple-element.21), channel_id=1, source_target_pairs={{0,1},{1,2},{2,3},{3,4},{4,5},{5,6},{6,7},{7,8},{8,9},{9,10},{10,1... | collective-permute-start | bytes 49160 | tf_op jit(solution)/shard_map/ppermute | solution.py:20
  189.6 7.2 %collective-permute-start.29 = (bf16[1,64,128]{2,1,0:T(8,128)(2,1)S(1)}, bf16[1,64,128]{2,1,0:T(8,128)(2,1)S(1)}, u32[]{:S(2)}, u32[]{:S(2)}) collective-permute-start(bf16[1,64,128]{2,1,0:T(8,128)(2,1)S(1)} %get-tuple-element.22), channel_id=1, source_target_pairs={{1,0},{2,1},{3,2},{4,3},{5,4},{6,5},{7,6},{8,7},{9,8},{10,9},{11,1... | collective-permute-start | bytes 49160 | tf_op jit(solution)/shard_map/ppermute | solution.py:22
  199.4 4.5 %collective-permute-start.30 = (bf16[1,128,128]{2,1,0:T(8,128)(2,1)S(1)}, bf16[1,128,128]{2,1,0:T(8,128)(2,1)S(1)}, u32[]{:S(2)}, u32[]{:S(2)}) collective-permute-start(bf16[1,128,128]{2,1,0:T(8,128)(2,1)S(1)} %get-tuple-element.13), channel_id=1, source_target_pairs={{0,1},{1,2},{2,3},{3,4},{4,5},{5,6},{6,7},{7,8},{8,9},{9,10},{10,1... | collective-permute-start | bytes 98312 | tf_op jit(solution)/shard_map/ppermute | solution.py:20
  201.3 7.6 %copy-start.3 = (bf16[3,3,128,128]{3,2,1,0:T(8,128)(2,1)S(1)}, bf16[3,3,128,128]{3,2,1,0:T(8,128)(2,1)}, u32[]{:S(2)}) copy-start(bf16[3,3,128,128]{3,2,1,0:T(8,128)(2,1)} %param.26) | copy-start | bytes 884740
  201.3 7.5 %collective-permute-start.31 = (bf16[1,128,128]{2,1,0:T(8,128)(2,1)S(1)}, bf16[1,128,128]{2,1,0:T(8,128)(2,1)S(1)}, u32[]{:S(2)}, u32[]{:S(2)}) collective-permute-start(bf16[1,128,128]{2,1,0:T(8,128)(2,1)S(1)} %get-tuple-element.14), channel_id=1, source_target_pairs={{1,0},{2,1},{3,2},{4,3},{5,4},{6,5},{7,6},{8,7},{9,8},{10,9},{11,1... | collective-permute-start | bytes 98312 | tf_op jit(solution)/shard_map/ppermute | solution.py:22
  211.0 4.4 %collective-permute-start.32 = (bf16[1,128,128]{2,1,0:T(8,128)(2,1)S(1)}, bf16[1,128,128]{2,1,0:T(8,128)(2,1)S(1)}, u32[]{:S(2)}, u32[]{:S(2)}) collective-permute-start(bf16[1,128,128]{2,1,0:T(8,128)(2,1)S(1)} %get-tuple-element.11), channel_id=1, source_target_pairs={{0,1},{1,2},{2,3},{3,4},{4,5},{5,6},{6,7},{7,8},{8,9},{9,10},{10,1... | collective-permute-start | bytes 98312 | tf_op jit(solution)/shard_map/ppermute | solution.py:20
  212.9 7.5 %copy-start.13 = (bf16[3,3,4,128]{3,2,1,0:T(4,128)(2,1)S(1)}, bf16[3,3,4,128]{3,2,1,0:T(4,128)(2,1)}, u32[]{:S(2)}) copy-start(bf16[3,3,4,128]{3,2,1,0:T(4,128)(2,1)} %param.27) | copy-start | bytes 27652
  212.9 7.3 %collective-permute-start.33 = (bf16[1,128,128]{2,1,0:T(8,128)(2,1)S(1)}, bf16[1,128,128]{2,1,0:T(8,128)(2,1)S(1)}, u32[]{:S(2)}, u32[]{:S(2)}) collective-permute-start(bf16[1,128,128]{2,1,0:T(8,128)(2,1)S(1)} %get-tuple-element.12), channel_id=1, source_target_pairs={{1,0},{2,1},{3,2},{4,3},{5,4},{6,5},{7,6},{8,7},{9,8},{10,9},{11,1... | collective-permute-start | bytes 98312 | tf_op jit(solution)/shard_map/ppermute | solution.py:22
  222.1 4.5 %collective-permute-start.34 = (bf16[20,1,128]{2,0,1:T(8,128)(2,1)S(1)}, bf16[20,1,128]{2,0,1:T(8,128)(2,1)S(1)}, u32[]{:S(2)}, u32[]{:S(2)}) collective-permute-start(bf16[20,1,128]{2,0,1:T(8,128)(2,1)S(1)} %get-tuple-element.25), channel_id=1, source_target_pairs={{0,1},{1,2},{2,3},{3,4},{4,5},{5,6},{6,7},{7,8},{8,9},{9,10},{10,1... | collective-permute-start | bytes 15368 | tf_op jit(solution)/shard_map/ppermute | solution.py:20
  224.1 7.1 %collective-permute-start.35 = (bf16[20,1,128]{2,0,1:T(8,128)(2,1)S(1)}, bf16[20,1,128]{2,0,1:T(8,128)(2,1)S(1)}, u32[]{:S(2)}, u32[]{:S(2)}) collective-permute-start(bf16[20,1,128]{2,0,1:T(8,128)(2,1)S(1)} %get-tuple-element.26), channel_id=1, source_target_pairs={{1,0},{2,1},{3,2},{4,3},{5,4},{6,5},{7,6},{8,7},{9,8},{10,9},{11,1... | collective-permute-start | bytes 15368 | tf_op jit(solution)/shard_map/ppermute | solution.py:22
  234.2 4.3 %collective-permute-start.36 = (bf16[1,128,128]{2,1,0:T(8,128)(2,1)S(1)}, bf16[1,128,128]{2,1,0:T(8,128)(2,1)S(1)}, u32[]{:S(2)}, u32[]{:S(2)}) collective-permute-start(bf16[1,128,128]{2,1,0:T(8,128)(2,1)S(1)} %get-tuple-element.9), channel_id=1, source_target_pairs={{0,1},{1,2},{2,3},{3,4},{4,5},{5,6},{6,7},{7,8},{8,9},{9,10},{10,1... | collective-permute-start | bytes 98312 | tf_op jit(solution)/shard_map/ppermute | solution.py:20
  236.2 7.3 %collective-permute-start.37 = (bf16[1,128,128]{2,1,0:T(8,128)(2,1)S(1)}, bf16[1,128,128]{2,1,0:T(8,128)(2,1)S(1)}, u32[]{:S(2)}, u32[]{:S(2)}) collective-permute-start(bf16[1,128,128]{2,1,0:T(8,128)(2,1)S(1)} %get-tuple-element.10), channel_id=1, source_target_pairs={{1,0},{2,1},{3,2},{4,3},{5,4},{6,5},{7,6},{8,7},{9,8},{10,9},{11,1... | collective-permute-start | bytes 98312 | tf_op jit(solution)/shard_map/ppermute | solution.py:22
  246.6 4.3 %collective-permute-start.38 = (bf16[1,64,128]{2,1,0:T(8,128)(2,1)S(1)}, bf16[1,64,128]{2,1,0:T(8,128)(2,1)S(1)}, u32[]{:S(2)}, u32[]{:S(2)}) collective-permute-start(bf16[1,64,128]{2,1,0:T(8,128)(2,1)S(1)} %get-tuple-element.19), channel_id=1, source_target_pairs={{0,1},{1,2},{2,3},{3,4},{4,5},{5,6},{6,7},{7,8},{8,9},{9,10},{10,1... | collective-permute-start | bytes 49160 | tf_op jit(solution)/shard_map/ppermute | solution.py:20
  248.5 7.2 %collective-permute-start.39 = (bf16[1,64,128]{2,1,0:T(8,128)(2,1)S(1)}, bf16[1,64,128]{2,1,0:T(8,128)(2,1)S(1)}, u32[]{:S(2)}, u32[]{:S(2)}) collective-permute-start(bf16[1,64,128]{2,1,0:T(8,128)(2,1)S(1)} %get-tuple-element.20), channel_id=1, source_target_pairs={{1,0},{2,1},{3,2},{4,3},{5,4},{6,5},{7,6},{8,7},{9,8},{10,9},{11,1... | collective-permute-start | bytes 49160 | tf_op jit(solution)/shard_map/ppermute | solution.py:22
  257.5 4.5 %collective-permute-start.40 = (bf16[1,64,128]{2,1,0:T(8,128)(2,1)S(1)}, bf16[1,64,128]{2,1,0:T(8,128)(2,1)S(1)}, u32[]{:S(2)}, u32[]{:S(2)}) collective-permute-start(bf16[1,64,128]{2,1,0:T(8,128)(2,1)S(1)} %get-tuple-element.17), channel_id=1, source_target_pairs={{0,1},{1,2},{2,3},{3,4},{4,5},{5,6},{6,7},{7,8},{8,9},{9,10},{10,1... | collective-permute-start | bytes 49160 | tf_op jit(solution)/shard_map/ppermute | solution.py:20
  259.4 7.2 %collective-permute-start.41 = (bf16[1,64,128]{2,1,0:T(8,128)(2,1)S(1)}, bf16[1,64,128]{2,1,0:T(8,128)(2,1)S(1)}, u32[]{:S(2)}, u32[]{:S(2)}) collective-permute-start(bf16[1,64,128]{2,1,0:T(8,128)(2,1)S(1)} %get-tuple-element.18), channel_id=1, source_target_pairs={{1,0},{2,1},{3,2},{4,3},{5,4},{6,5},{7,6},{8,7},{9,8},{10,9},{11,1... | collective-permute-start | bytes 49160 | tf_op jit(solution)/shard_map/ppermute | solution.py:22
  269.2 4.3 %collective-permute-start.42 = (bf16[1,128,128]{2,1,0:T(8,128)(2,1)S(1)}, bf16[1,128,128]{2,1,0:T(8,128)(2,1)S(1)}, u32[]{:S(2)}, u32[]{:S(2)}) collective-permute-start(bf16[1,128,128]{2,1,0:T(8,128)(2,1)S(1)} %get-tuple-element.7), channel_id=1, source_target_pairs={{0,1},{1,2},{2,3},{3,4},{4,5},{5,6},{6,7},{7,8},{8,9},{9,10},{10,1... | collective-permute-start | bytes 98312 | tf_op jit(solution)/shard_map/ppermute | solution.py:20
  271.1 7.3 %collective-permute-start.43 = (bf16[1,128,128]{2,1,0:T(8,128)(2,1)S(1)}, bf16[1,128,128]{2,1,0:T(8,128)(2,1)S(1)}, u32[]{:S(2)}, u32[]{:S(2)}) collective-permute-start(bf16[1,128,128]{2,1,0:T(8,128)(2,1)S(1)} %get-tuple-element.8), channel_id=1, source_target_pairs={{1,0},{2,1},{3,2},{4,3},{5,4},{6,5},{7,6},{8,7},{9,8},{10,9},{11,1... | collective-permute-start | bytes 98312 | tf_op jit(solution)/shard_map/ppermute | solution.py:22
  280.7 4.3 %collective-permute-start.44 = (bf16[1,128,128]{2,1,0:T(8,128)(2,1)S(1)}, bf16[1,128,128]{2,1,0:T(8,128)(2,1)S(1)}, u32[]{:S(2)}, u32[]{:S(2)}) collective-permute-start(bf16[1,128,128]{2,1,0:T(8,128)(2,1)S(1)} %get-tuple-element.5), channel_id=1, source_target_pairs={{0,1},{1,2},{2,3},{3,4},{4,5},{5,6},{6,7},{7,8},{8,9},{9,10},{10,1... | collective-permute-start | bytes 98312 | tf_op jit(solution)/shard_map/ppermute | solution.py:20
  282.6 7.3 %collective-permute-start.45 = (bf16[1,128,128]{2,1,0:T(8,128)(2,1)S(1)}, bf16[1,128,128]{2,1,0:T(8,128)(2,1)S(1)}, u32[]{:S(2)}, u32[]{:S(2)}) collective-permute-start(bf16[1,128,128]{2,1,0:T(8,128)(2,1)S(1)} %get-tuple-element.6), channel_id=1, source_target_pairs={{1,0},{2,1},{3,2},{4,3},{5,4},{6,5},{7,6},{8,7},{9,8},{10,9},{11,1... | collective-permute-start | bytes 98312 | tf_op jit(solution)/shard_map/ppermute | solution.py:22
